TPU v7x, 512 devices: a whole 4x4x16 slice. The times are simulated.
512 devices in a mesh: ingest: 8 (over y, core), owner: 64 (over x, z).
Axes of the slice: x: 4, y: 4, z: 16, core: 2. Of those that a mesh axis runs over, the one named last changes fastest.
Arguments:
- frame_rows: bfloat16 [2112, 28, 1024], P('owner', None, 'ingest'), may hold values from -32 to 32
- route_owner: int32 [2112], P('owner'), may hold values from 0 to 63, as said below
- route_slot: int32 [2112], P('owner'), may hold values from 0 to 32, as said below
- frames: int32 [2112], P('owner'), may hold values from 1 to 28, as said below
- kv_cache: bfloat16 [2112, 8, 70, 256], P('owner', 'ingest'), may hold values from -250 to 250
- conv_cache: bfloat16 [2112, 8, 1024], P('owner', None, 'ingest'), may hold values from -5 to 5
- mig_owner: int32 [2048], P('owner'), may hold values from 0 to 63, as said below
- ln1_gain: float32 [1024], replicated, may hold values from 0.1 to 1.9
- w_qkv: bfloat16 [1024, 8, 384], P(None, 'ingest'), may hold values from -0.1875 to 0.1875
- w_out: bfloat16 [1024, 1024], P('ingest'), may hold values from -0.1875 to 0.1875
- ln2_gain: float32 [1024], replicated, may hold values from 0.1 to 1.9
- w_pw1: bfloat16 [1024, 2, 1024], P(None, None, 'ingest'), may hold values from -0.1875 to 0.1875
- dw_weight: bfloat16 [9, 1024], P(None, 'ingest'), may hold values from -2 to 2
- bn_scale: float32 [1024], P('ingest'), may hold values from 0.1 to 1.9
- bn_shift: float32 [1024], P('ingest'), may hold values from -2.5 to 2.5
- w_pw2: bfloat16 [1024, 1024], P('ingest'), may hold values from -0.1875 to 0.1875
Outputs:
- layer_out: bfloat16 [2112, 28, 1024], P('owner', None, 'ingest')
- kv_next: bfloat16 [2112, 8, 70, 256], P('owner', 'ingest')
- conv_next: bfloat16 [2112, 8, 1024], P('owner', None, 'ingest')
Inputs may be any that keep to these rules, and one draw needn't show every extreme that they name: `route_owner`: every owner receives exactly 33 utterances. The utterances that one source device along owner (a block of 33 rows in arrival order) sends to one owner number at most 1, and some source device reaches that number. `route_slot`: the utterances sent to one owner have distinct slots. Every owner holds an utterance with 28 new frames. The utterance in old slot 1 + j of an owner moves to slot 1 + j of owner mig_owner; the 32 utterances of one owner go to 32 different other owners, and every owner receives exactly one utterance for each j.
All inputs are finite; a program needn't handle non-finite values.
Results may differ from a plain program's by a relative error of at most 0.01.
Values may be sent and summed in bfloat16 or wider, within the bound.
No kernel may reach another device: no remote copies, remote signals or barrier semaphores. Data moves between devices by JAX's collectives and lax.ppermute only.
A program may use at most 64 MiB of HBM per device.

v0:
```python
import jax
import jax.numpy as jnp
from jax import lax
from jax.sharding import PartitionSpec as P

BLOCKS = 2


norm_eps = 1e-05


def normalize(values, gain_cols):
    model_width = values.shape[-1]
    row_mean = jnp.sum(values, axis=-1, keepdims=True) / model_width
    spread = jnp.sum(values * values, axis=-1, keepdims=True) / model_width - row_mean * row_mean
    return ((values - row_mean) * lax.rsqrt(spread + norm_eps) * gain_cols).astype(jnp.bfloat16)


def one_hot_rows(table, rows):
    return jnp.dot(
        table.astype(jnp.bfloat16), rows, preferred_element_type=jnp.float32
    ).astype(jnp.bfloat16)


def grouped_terms(left_groups, right_groups):
    terms = jnp.einsum(
        "grc,gcn->grn", left_groups, right_groups, preferred_element_type=jnp.float32
    ).astype(jnp.bfloat16)
    return jnp.sum(terms.astype(jnp.float32), axis=0)


def shards(
    frame_rows,
    route_owner,
    route_slot,
    frames,
    kv_cache,
    conv_cache,
    mig_owner,
    ln1_gain,
    w_qkv,
    w_out,
    ln2_gain,
    w_pw1,
    dw_weight,
    bn_scale,
    bn_shift,
    w_pw2,
):
    owners = lax.axis_size("owner")
    groups = lax.axis_size("ingest")
    me = lax.axis_index("ingest")
    utterances, frame_span, local_width = frame_rows.shape
    model_width = w_qkv.shape[0]
    head_dim = w_qkv.shape[2] // 3
    cache_len = kv_cache.shape[2]
    conv_len = conv_cache.shape[1]
    taps = dw_weight.shape[0]
    horizon = frame_span // BLOCKS
    moving = mig_owner.shape[0]
    settled = utterances - moving
    lanes = 128

    w_out_full = lax.all_gather(w_out, "ingest", axis=0, tiled=True)
    w_pw2_cols = lax.all_to_all(
        w_pw2.reshape(local_width, groups, local_width).transpose(1, 0, 2),
        "ingest",
        split_axis=0,
        concat_axis=0,
        tiled=True,
    )

    dest = jnp.arange(owners, dtype=jnp.int32)
    frame_flat = frame_rows.reshape(utterances, frame_span * local_width)
    slot_tag = jnp.broadcast_to(
        (route_slot + 1).astype(jnp.bfloat16)[:, None], (utterances, lanes)
    )
    frame_send = one_hot_rows(
        dest[:, None] == route_owner[None, :], jnp.concatenate([frame_flat, slot_tag], axis=1)
    )
    kv_width = cache_len * 2 * head_dim
    conv_width = conv_len * local_width
    mover_tag = jnp.broadcast_to(
        (jnp.arange(moving, dtype=jnp.int32) + 1).astype(jnp.bfloat16)[:, None], (moving, lanes)
    )
    cache_rows = jnp.concatenate(
        [
            kv_cache[settled:].reshape(moving, kv_width),
            conv_cache[settled:].reshape(moving, conv_width),
            mover_tag,
        ],
        axis=1,
    )
    cache_send = one_hot_rows(dest[:, None] == mig_owner[None, :], cache_rows)
    frame_cols = frame_send.shape[1]
    arrived = lax.all_to_all(
        jnp.concatenate([frame_send, cache_send], axis=1),
        "owner",
        split_axis=0,
        concat_axis=0,
        tiled=True,
    )
    frame_part = frame_span * local_width
    got_slot = arrived[:, frame_part].astype(jnp.int32)
    slots = jnp.arange(utterances, dtype=jnp.int32)
    arranged = one_hot_rows(
        slots[:, None] + 1 == got_slot[None, :], arrived[:, :frame_part]
    ).reshape(utterances, frame_span, local_width)
    got_mover = arrived[:, frame_cols + kv_width + conv_width].astype(jnp.int32)
    movers = jnp.arange(moving, dtype=jnp.int32)
    moved = one_hot_rows(
        movers[:, None] + 1 == got_mover[None, :],
        arrived[:, frame_cols : frame_cols + kv_width + conv_width],
    )
    kv_state = jnp.concatenate(
        [
            kv_cache[:settled].reshape(settled, cache_len, 2 * head_dim),
            moved[:, :kv_width].reshape(moving, cache_len, 2 * head_dim),
        ],
        axis=0,
    )
    conv_state = jnp.concatenate(
        [conv_cache[:settled], moved[:, kv_width:].reshape(moving, conv_len, local_width)],
        axis=0,
    )

    x_all = lax.all_gather(arranged, "ingest", axis=0, tiled=False)
    x_rows = x_all.transpose(1, 2, 0, 3).reshape(utterances, frame_span, model_width)
    x_rows = x_rows.astype(jnp.float32)
    normed = normalize(x_rows, ln1_gain)
    projected = jnp.dot(
        normed, w_qkv.reshape(model_width, 3 * head_dim), preferred_element_type=jnp.float32
    )
    queries = projected[..., :head_dim].astype(jnp.bfloat16)
    fresh = projected[..., head_dim:].astype(jnp.bfloat16)

    memory = jnp.concatenate([kv_state, fresh], axis=1)
    keys_total = memory.shape[1]
    scores = jnp.einsum(
        "sqd,skd->sqk", queries, memory[..., :head_dim], preferred_element_type=jnp.float32
    ) * head_dim ** (-0.5)
    frame_index = jnp.arange(frame_span, dtype=jnp.int32)
    block_of = frame_index // horizon
    low = block_of * horizon
    high = cache_len + jnp.minimum(frames[:, None], (block_of[None, :] + 1) * horizon)
    position = jnp.arange(keys_total, dtype=jnp.int32)
    live_keys = (position[None, None, :] >= low[None, :, None]) & (
        position[None, None, :] < high[:, :, None]
    )
    scores = jnp.where(live_keys, scores, -1e30)
    row_max = jnp.max(scores, axis=-1, keepdims=True)
    weights = jnp.exp(scores - row_max)
    probabilities = (weights / jnp.sum(weights, axis=-1, keepdims=True)).astype(jnp.bfloat16)
    context = jnp.einsum(
        "sqk,skd->sqd", probabilities, memory[..., head_dim:], preferred_element_type=jnp.float32
    ).astype(jnp.bfloat16)

    ctx_all = lax.all_gather(context, "ingest", axis=0, tiled=False)
    row_count = utterances * frame_span
    attn = grouped_terms(
        ctx_all.reshape(groups, row_count, head_dim),
        w_out_full.reshape(groups, head_dim, model_width),
    )
    residual = x_rows.reshape(row_count, model_width) + attn
    normed2 = normalize(residual, ln2_gain)
    mixed = jnp.dot(
        normed2, w_pw1.reshape(model_width, 2 * local_width), preferred_element_type=jnp.float32
    )
    glu_out = (mixed[:, :local_width] * jax.nn.sigmoid(mixed[:, local_width:])).astype(
        jnp.bfloat16
    )
    glu_out = glu_out.reshape(utterances, frame_span, local_width)

    joined = jnp.concatenate([conv_state, glu_out], axis=1)
    joined_f = joined.astype(jnp.float32)
    running = jnp.zeros((utterances, frame_span, local_width), jnp.float32)
    for tap_index in range(taps):
        running = running + joined_f[:, tap_index : tap_index + frame_span, :] * dw_weight[
            tap_index
        ].astype(jnp.float32)
    activated = jax.nn.silu(running * bn_scale + bn_shift).astype(jnp.bfloat16)

    act_all = lax.all_gather(activated, "ingest", axis=0, tiled=False)
    conv_terms = grouped_terms(act_all.reshape(groups, row_count, local_width), w_pw2_cols)
    residual_own = lax.dynamic_slice_in_dim(residual, me * local_width, local_width, 1)
    result = (residual_own + conv_terms).reshape(utterances, frame_span, local_width)
    live_rows = frame_index[None, :] < frames[:, None]
    layer_out = jnp.where(live_rows[:, :, None], result, 0.0).astype(jnp.bfloat16)

    keep = jnp.arange(cache_len, dtype=jnp.int32)
    kv_pick = position[None, None, :] == keep[None, :, None] + frames[:, None, None]
    kv_next = jnp.einsum(
        "srp,spd->srd", kv_pick.astype(jnp.bfloat16), memory, preferred_element_type=jnp.float32
    ).astype(jnp.bfloat16)
    conv_keep = jnp.arange(conv_len, dtype=jnp.int32)
    conv_pos = jnp.arange(joined.shape[1], dtype=jnp.int32)
    conv_pick = conv_pos[None, None, :] == conv_keep[None, :, None] + frames[:, None, None]
    conv_next = jnp.einsum(
        "srp,spd->srd", conv_pick.astype(jnp.bfloat16), joined, preferred_element_type=jnp.float32
    ).astype(jnp.bfloat16)
    return (layer_out, kv_next.reshape(kv_cache.shape), conv_next)


def solution(mesh):
    in_specs = (
        P("owner", None, "ingest"),
        P("owner"),
        P("owner"),
        P("owner"),
        P("owner", "ingest", None, None),
        P("owner", None, "ingest"),
        P("owner"),
        P(),
        P(None, "ingest", None),
        P("ingest", None),
        P(),
        P(None, None, "ingest"),
        P(None, "ingest"),
        P("ingest"),
        P("ingest"),
        P("ingest", None),
    )
    out_specs = (
        P("owner", None, "ingest"),
        P("owner", "ingest", None, None),
        P("owner", None, "ingest"),
    )
    return jax.shard_map(shards, mesh=mesh, in_specs=in_specs, out_specs=out_specs, check_vma=False)
```

profile of v0, /device:TPU:1, one launch (start us, length us, event | category | flops | bytes accessed | tf_op | source)
XLA Modules:
  0.0 387.9 jit_solution(17638379592714041639)
XLA Ops:
  12.8 5.4 %reduce.8 = bf16[64,22784]{1,0:T(8,128)(2,1)} reduce(bf16[64,1,22784]{2,0,1:T(8,128)(2,1)} %maximum_bitcast_fusion, bf16[]{:T(256)} %broadcast.254), dimensions={1}, to_apply=%copy.30.reduce_sub_computation | reduce | bytes 5832706 | tf_op jit(solution)/shard_map/all_to_all | solution.py:96
  18.2 4.4 %reshape.407 = bf16[64,2,11392]{2,1,0:T(2,128)(2,1)} reshape(bf16[64,22784]{1,0:T(8,128)(2,1)} %reduce.8) | data formatting | bytes 5832704
  22.6 19.3 %all-to-all-start = ((bf16[64,2,11392]{2,1,0:T(2,128)(2,1)}), bf16[64,2,11392]{2,1,0:T(2,128)(2,1)}, u32[]{:S(2)}, u32[]{:S(2)}) async-start(bf16[64,2,11392]{2,1,0:T(2,128)(2,1)} %reshape.407), calls=%async_computation | async-start | bytes 5832704 | tf_op jit(solution)/shard_map/all_to_all | solution.py:96
  42.0 127.4 %all-to-all-done = bf16[64,2,11392]{2,1,0:T(2,128)(2,1)} async-done(((bf16[64,2,11392]{2,1,0:T(2,128)(2,1)}), bf16[64,2,11392]{2,1,0:T(2,128)(2,1)}, u32[]{:S(2)}, u32[]{:S(2)}) %all-to-all-start) | async-done | bytes 2916384 | tf_op jit(solution)/shard_map/all_to_all | solution.py:96
  169.5 16.8 %reshape.408 = bf16[64,1,22784]{2,1,0:T(2,128)(2,1)} reshape(bf16[64,2,11392]{2,1,0:T(2,128)(2,1)} %all-to-all-done) | data formatting | bytes 5832704
  186.2 3.1 copy.57
  192.5 2.2 convolution_convert_fusion.1
  195.9 2.5 reshape.378
  198.4 26.5 %all-gather.7.cloned.1.call-done = bf16[8,33,28,128]{3,2,1,0:T(8,128)(2,1)} async-done(((bf16[1,33,28,128]{3,2,1,0:T(8,128)(2,1)}), bf16[8,33,28,128]{3,2,1,0:T(8,128)(2,1)}) %all-gather.7.cloned.1.call-update) | async-done | bytes 1892368 | tf_op jit(solution)/shard_map/all_gather | solution.py:127
  224.9 5.3 %bitcast_reduce_fusion = (f32[33,28]{1,0:T(8,128)S(1)}, f32[33,28]{1,0:T(8,128)S(1)}) fusion(bf16[8,33,28,128]{3,2,1,0:T(8,128)(2,1)} %all-gather.7.cloned.1.call-done), kind=kLoop, calls=%fused_computation.9 | loop fusion | flops 3782856 | bytes 1899744 | tf_op jit(solution)/shard_map/reduce_sum | solution.py:14
  230.3 5.5 %fusion.3 = bf16[33,28,8,128]{3,2,1,0:T(8,128)(2,1)} fusion(f32[8,128]{1,0:T(8,128)S(1)} %bitcast.128, f32[33,28]{1,0:T(8,128)S(1)} %get-tuple-element.24, f32[33,28]{1,0:T(8,128)S(1)} %get-tuple-element.23, bf16[8,33,28,128]{3,2,1,0:T(8,128)(2,1)S(1)} %copy-done.2), kind=kLoop, calls=%fused_computation.13 | loop fusion | flops 4730880 | bytes 3796192 | tf_op jit(solution)/shard_map/convert_element_type | solution.py:16
  235.7 4.1 %convert_element_type.219 = bf16[33,28,1024]{2,1,0:T(8,128)(2,1)} reshape(bf16[33,28,8,128]{3,2,1,0:T(8,128)(2,1)} %fusion.3) | data formatting | bytes 3784704 | tf_op jit(solution)/shard_map/convert_element_type | solution.py:16
  239.9 3.0 convolution_convert_fusion.5
  245.5 3.8 convolution_convert_fusion.6
  251.8 31.2 %all-gather.11.cloned.1.call-done = bf16[264,28,128]{2,1,0:T(8,128)(2,1)} async-done(((bf16[33,28,128]{2,1,0:T(8,128)(2,1)}), bf16[264,28,128]{2,1,0:T(8,128)(2,1)}) %all-gather.11.cloned.1.call-update) | async-done | bytes 1892368 | tf_op jit(solution)/shard_map/all_gather | solution.py:158
  283.0 3.6 reshape.379
  286.6 32.0 %all-gather.9.cloned.1.call-done = bf16[1024,1024]{1,0:T(8,128)(2,1)} async-done(((bf16[128,1024]{1,0:T(8,128)(2,1)}), bf16[1024,1024]{1,0:T(8,128)(2,1)}) %all-gather.9.cloned.1.call-update) | async-done | bytes 2097168 | tf_op jit(solution)/shard_map/all_gather | solution.py:64
  318.6 6.6 %convert_reduce_fusion = f32[924,1024]{1,0:T(8,128)S(1)} fusion(bf16[8,924,128]{2,1,0:T(8,128)(2,1)} %reshape.379, bf16[8,128,1024]{2,1,0:T(8,128)(2,1)} %bitcast.129), kind=kOutput, calls=%fused_computation.1 | convolution fusion | flops 1959530496 | bytes 7774208 | tf_op jit(solution)/shard_map/grc,gcn->grn/dot_general | solution.py:26
  327.5 3.6 fusion.6
  331.1 5.0 %multiply_convert_fusion = bf16[33,28,8,128]{3,2,1,0:T(8,128)(2,1)S(1)} fusion(f32[8,128]{1,0:T(8,128)S(1)} %bitcast.127, f32[33,28]{1,0:T(8,128)S(1)} %get-tuple-element.22, f32[33,28]{1,0:T(8,128)S(1)} %get-tuple-element.21, f32[33,28,8,128]{3,2,1,0:T(8,128)S(1)} %bitcast.106, bf16[8,33,28,128]{3,2,1,0:T(8,128)(2,1)S(1)} %copy-done.2), kind=kLoop, calls=%fused_computation.15 | loop fusion | flops 5677056 | bytes 7580896 | tf_op jit(solution)/shard_map/convert_element_type | solution.py:16
  343.4 4.3 %all-to-all-start.1 = ((bf16[8,128,128]{2,1,0:T(8,128)(2,1)}), bf16[8,128,128]{2,1,0:T(8,128)(2,1)}, u32[]{:S(2)}, u32[]{:S(2)}) async-start(bf16[8,128,128]{2,1,0:T(8,128)(2,1)} %bitcast.18), calls=%async_computation.1 | async-start | bytes 524288 | tf_op jit(solution)/shard_map/all_to_all | solution.py:65
  351.4 2.8 copy.39
  355.0 19.9 %all-gather.13.cloned.1.call-done = bf16[264,28,128]{2,1,0:T(8,128)(2,1)} async-done(((bf16[33,28,128]{2,1,0:T(8,128)(2,1)}), bf16[264,28,128]{2,1,0:T(8,128)(2,1)}) %all-gather.13.cloned.1.call-update) | async-done | bytes 1892368 | tf_op jit(solution)/shard_map/all_gather | solution.py:183
  374.9 2.5 reshape.384
  (121 shorter events, 32.6 us)
Async XLA Ops:
  7.2 232.7 %copy-start = (bf16[1024,1,384]{2,0,1:T(8,128)(2,1)S(1)}, bf16[1024,1,384]{2,0,1:T(8,128)(2,1)}, u32[]{:S(2)}) copy-start(bf16[1024,1,384]{2,0,1:T(8,128)(2,1)} %param.24) | copy-start | bytes 2359300
  7.2 2.0 copy-start.26
  7.2 2.1 copy-start.23
  7.3 2.5 copy-start.24
  22.6 146.9 %all-to-all-start = ((bf16[64,2,11392]{2,1,0:T(2,128)(2,1)}), bf16[64,2,11392]{2,1,0:T(2,128)(2,1)}, u32[]{:S(2)}, u32[]{:S(2)}) async-start(bf16[64,2,11392]{2,1,0:T(2,128)(2,1)} %reshape.407), calls=%async_computation | async-start | bytes 5832704 | tf_op jit(solution)/shard_map/all_to_all | solution.py:96
  42.0 182.9 %all-gather.7.cloned.1.call-start = ((), (), s32[]{:S(2)}) async-start(), calls=%async_computation.2 | async-start | bytes 2433024 | tf_op jit(solution)/shard_map/all_gather | solution.py:127
  186.2 6.2 %copy-start.13 = (s32[33]{0:T(128)S(1)}, s32[33]{0:T(128)}, u32[]{:S(2)}) copy-start(s32[33]{0:T(128)} %param.19) | copy-start | bytes 400
  186.2 6.2 %copy-start.8 = (bf16[33,1,70,256]{3,2,1,0:T(8,128)(2,1)S(1)}, bf16[33,1,70,256]{3,2,1,0:T(8,128)(2,1)}, u32[]{:S(2)}) copy-start(bf16[33,1,70,256]{3,2,1,0:T(8,128)(2,1)} %param.20) | copy-start | bytes 3548164
  192.1 90.9 %all-gather.11.cloned.1.call-start = ((), (), s32[]{:S(2)}) async-start(), calls=%async_computation.4 | async-start | bytes 2433024 | tf_op jit(solution)/shard_map/all_gather | solution.py:158
  194.7 3.7 copy-start.4
  195.9 34.4 %copy-start.16 = (f32[1024]{0:T(1024)S(1)}, f32[1024]{0:T(1024)}, u32[]{:S(2)}) copy-start(f32[1024]{0:T(1024)} %param.23) | copy-start | bytes 12292
  224.9 5.4 %copy-start.2 = (bf16[8,33,28,128]{3,2,1,0:T(8,128)(2,1)S(1)}, bf16[8,33,28,128]{3,2,1,0:T(8,128)(2,1)}, u32[]{:S(2)}) copy-start(bf16[8,33,28,128]{3,2,1,0:T(8,128)(2,1)} %all-gather.7.cloned.1.call-done) | copy-start | bytes 5677060
  239.9 3.1 copy-start.6
  245.1 5.2 %copy-start.12 = (bf16[33,8,128]{2,1,0:T(8,128)(2,1)S(1)}, bf16[33,8,128]{2,1,0:T(8,128)(2,1)}, u32[]{:S(2)}) copy-start(bf16[33,8,128]{2,1,0:T(8,128)(2,1)} %param.21) | copy-start | bytes 202756
  245.1 5.2 %copy-start.14 = (bf16[9,128]{1,0:T(8,128)(2,1)S(1)}, bf16[9,128]{1,0:T(8,128)(2,1)}, u32[]{:S(2)}) copy-start(bf16[9,128]{1,0:T(8,128)(2,1)} %param.28) | copy-start | bytes 6916
  249.3 69.4 %all-gather.9.cloned.1.call-start = ((), (), s32[]{:S(2)}) async-start(), calls=%async_computation.3 | async-start | bytes 2359296 | tf_op jit(solution)/shard_map/all_gather | solution.py:64
  250.0 124.9 %all-gather.13.cloned.1.call-start = ((), (), s32[]{:S(2)}) async-start(), calls=%async_computation.5 | async-start | bytes 2433024 | tf_op jit(solution)/shard_map/all_gather | solution.py:183
  327.4 3.6 copy-start.15
  338.0 2.0 copy-start.17
  338.0 2.0 copy-start.18
  338.0 2.0 copy-start.19
  343.4 34.0 %all-to-all-start.1 = ((bf16[8,128,128]{2,1,0:T(8,128)(2,1)}), bf16[8,128,128]{2,1,0:T(8,128)(2,1)}, u32[]{:S(2)}, u32[]{:S(2)}) async-start(bf16[8,128,128]{2,1,0:T(8,128)(2,1)} %bitcast.18), calls=%async_computation.1 | async-start | bytes 524288 | tf_op jit(solution)/shard_map/all_to_all | solution.py:65
  351.3 2.8 copy-start.10
  374.9 6.4 %copy-start.1 = (bf16[1024,1,384]{2,0,1:T(8,128)(2,1)S(1)}, bf16[1024,1,384]{2,0,1:T(8,128)(2,1)}, u32[]{:S(2)}) copy-start(bf16[1024,1,384]{2,0,1:T(8,128)(2,1)} %param.24) | copy-start | bytes 2359300
  (11 other events, 18.3 us)
Sparse Core Ops, SparseCore 0:
  192.2 32.6 all-gather.6
  249.4 33.5 all-gather.10
  285.2 33.4 all-gather.8
  341.5 33.3 all-gather.12
where the time goes:
time: 389 us; the launch traced here: 388 us
  waiting for transfers between devices  238 us (61%)
  local copies, waits for them, and re-layouts  54.9 us (14%)
  other arithmetic  34 us (9%)
  starting transfers between devices  24.2 us (6%)
  matrix products  22.6 us (6%)
  between operations  14.4 us (4%)
    all_to_all x1, waiting for transfers between devices, shards(): lax.all_to_all(jnp.concatenate([frame_send, cache_send], axis=1), 'owner'...  127 us
    unnamed x70, local copies, waits for them, and re-layouts  36.2 us
    all_gather x1, waiting for transfers between devices, shards(): w_out_full = lax.all_gather(w_out, 'ingest', axis=0, tiled=True)  32 us
    all_gather x1, waiting for transfers between devices, shards(): ctx_all = lax.all_gather(context, 'ingest', axis=0, tiled=False)  31.2 us
    all_gather x1, waiting for transfers between devices, shards(): x_all = lax.all_gather(arranged, 'ingest', axis=0, tiled=False)  26.5 us
    all_gather x1, waiting for transfers between devices, shards(): act_all = lax.all_gather(activated, 'ingest', axis=0, tiled=False)  19.9 us
    all_to_all x1, starting transfers between devices, shards(): lax.all_to_all(jnp.concatenate([frame_send, cache_send], axis=1), 'owner'...  19.3 us
    convert_element_type x2, other arithmetic, normalize(): ((values - row_mean) * lax.rsqrt(spread + norm_eps) * gain_cols).astype(j...  10.5 us
  transfers between devices with their start and end apart: 6, of which 5 were waited for; matrix products, arithmetic and copies ran while one was open for 6% of the time, Pallas kernels for 0%

commit v1 on v0

--- a/solution.py
+++ b/solution.py
@@ -14,19 +14,6 @@
     row_mean = jnp.sum(values, axis=-1, keepdims=True) / model_width
     spread = jnp.sum(values * values, axis=-1, keepdims=True) / model_width - row_mean * row_mean
     return ((values - row_mean) * lax.rsqrt(spread + norm_eps) * gain_cols).astype(jnp.bfloat16)
-
-
-def one_hot_rows(table, rows):
-    return jnp.dot(
-        table.astype(jnp.bfloat16), rows, preferred_element_type=jnp.float32
-    ).astype(jnp.bfloat16)
-
-
-def grouped_terms(left_groups, right_groups):
-    terms = jnp.einsum(
-        "grc,gcn->grn", left_groups, right_groups, preferred_element_type=jnp.float32
-    ).astype(jnp.bfloat16)
-    return jnp.sum(terms.astype(jnp.float32), axis=0)
 
 
 def shards(
@@ -59,72 +46,66 @@
     horizon = frame_span // BLOCKS
     moving = mig_owner.shape[0]
     settled = utterances - moving
-    lanes = 128
-
-    w_out_full = lax.all_gather(w_out, "ingest", axis=0, tiled=True)
-    w_pw2_cols = lax.all_to_all(
-        w_pw2.reshape(local_width, groups, local_width).transpose(1, 0, 2),
-        "ingest",
-        split_axis=0,
-        concat_axis=0,
-        tiled=True,
-    )
 
     dest = jnp.arange(owners, dtype=jnp.int32)
-    frame_flat = frame_rows.reshape(utterances, frame_span * local_width)
+    frame_pad = -(-(frame_span + 1) // 16) * 16
     slot_tag = jnp.broadcast_to(
-        (route_slot + 1).astype(jnp.bfloat16)[:, None], (utterances, lanes)
-    )
-    frame_send = one_hot_rows(
-        dest[:, None] == route_owner[None, :], jnp.concatenate([frame_flat, slot_tag], axis=1)
-    )
-    kv_width = cache_len * 2 * head_dim
-    conv_width = conv_len * local_width
+        (route_slot + 1).astype(jnp.bfloat16)[:, None, None], (utterances, 1, local_width)
+    )
+    frame_rows_tagged = jnp.concatenate(
+        [
+            frame_rows,
+            slot_tag,
+            jnp.zeros((utterances, frame_pad - frame_span - 1, local_width), jnp.bfloat16),
+        ],
+        axis=1,
+    )
+    frame_send = jnp.einsum(
+        "ds,stc->dtc",
+        (dest[:, None] == route_owner[None, :]).astype(jnp.bfloat16),
+        frame_rows_tagged,
+        preferred_element_type=jnp.float32,
+    ).astype(jnp.bfloat16)
+    frame_got = lax.all_to_all(frame_send, "owner", split_axis=0, concat_axis=0, tiled=True)
+
+    kv_lanes = 2 * head_dim
+    conv_fold = conv_len * local_width // kv_lanes
+    cache_used = cache_len + conv_fold + 1
+    cache_pad = -(-cache_used // 16) * 16
     mover_tag = jnp.broadcast_to(
-        (jnp.arange(moving, dtype=jnp.int32) + 1).astype(jnp.bfloat16)[:, None], (moving, lanes)
+        (jnp.arange(moving, dtype=jnp.int32) + 1).astype(jnp.bfloat16)[:, None, None],
+        (moving, 1, kv_lanes),
     )
     cache_rows = jnp.concatenate(
         [
-            kv_cache[settled:].reshape(moving, kv_width),
-            conv_cache[settled:].reshape(moving, conv_width),
+            kv_cache[settled:, 0],
+            conv_cache[settled:].reshape(moving, conv_fold, kv_lanes),
             mover_tag,
+            jnp.zeros((moving, cache_pad - cache_used, kv_lanes), jnp.bfloat16),
         ],
         axis=1,
     )
-    cache_send = one_hot_rows(dest[:, None] == mig_owner[None, :], cache_rows)
-    frame_cols = frame_send.shape[1]
-    arrived = lax.all_to_all(
-        jnp.concatenate([frame_send, cache_send], axis=1),
-        "owner",
-        split_axis=0,
-        concat_axis=0,
-        tiled=True,
-    )
-    frame_part = frame_span * local_width
-    got_slot = arrived[:, frame_part].astype(jnp.int32)
+    cache_send = jnp.einsum(
+        "dj,jrc->drc",
+        (dest[:, None] == mig_owner[None, :]).astype(jnp.bfloat16),
+        cache_rows,
+        preferred_element_type=jnp.float32,
+    ).astype(jnp.bfloat16)
+    cache_got = lax.all_to_all(cache_send, "owner", split_axis=0, concat_axis=0, tiled=True)
+
+    got_slot = frame_got[:, frame_span, 0].astype(jnp.int32)
     slots = jnp.arange(utterances, dtype=jnp.int32)
-    arranged = one_hot_rows(
-        slots[:, None] + 1 == got_slot[None, :], arrived[:, :frame_part]
-    ).reshape(utterances, frame_span, local_width)
-    got_mover = arrived[:, frame_cols + kv_width + conv_width].astype(jnp.int32)
-    movers = jnp.arange(moving, dtype=jnp.int32)
-    moved = one_hot_rows(
-        movers[:, None] + 1 == got_mover[None, :],
-        arrived[:, frame_cols : frame_cols + kv_width + conv_width],
-    )
-    kv_state = jnp.concatenate(
-        [
-            kv_cache[:settled].reshape(settled, cache_len, 2 * head_dim),
-            moved[:, :kv_width].reshape(moving, cache_len, 2 * head_dim),
-        ],
-        axis=0,
-    )
-    conv_state = jnp.concatenate(
-        [conv_cache[:settled], moved[:, kv_width:].reshape(moving, conv_len, local_width)],
-        axis=0,
-    )
+    arranged = jnp.einsum(
+        "so,otc->stc",
+        (slots[:, None] + 1 == got_slot[None, :]).astype(jnp.bfloat16),
+        frame_got[:, :frame_span],
+        preferred_element_type=jnp.float32,
+    ).astype(jnp.bfloat16)
 
     x_all = lax.all_gather(arranged, "ingest", axis=0, tiled=False)
+    w_out_in, w_pw2_in, x_all = lax.optimization_barrier((w_out, w_pw2, x_all))
+    w_out_full = lax.all_gather(w_out_in, "ingest", axis=0, tiled=True)
+    w_pw2_full = lax.all_gather(w_pw2_in, "ingest", axis=0, tiled=True)
     x_rows = x_all.transpose(1, 2, 0, 3).reshape(utterances, frame_span, model_width)
     x_rows = x_rows.astype(jnp.float32)
     normed = normalize(x_rows, ln1_gain)
@@ -133,6 +114,26 @@
     )
     queries = projected[..., :head_dim].astype(jnp.bfloat16)
     fresh = projected[..., head_dim:].astype(jnp.bfloat16)
+    w_out_full, w_pw2_full, queries, fresh = lax.optimization_barrier(
+        (w_out_full, w_pw2_full, queries, fresh)
+    )
+    w_pw2_cols = lax.dynamic_slice_in_dim(w_pw2_full, me * local_width, local_width, 1).reshape(
+        groups, local_width, local_width
+    )
+
+    got_mover = cache_got[:, cache_used - 1, 0].astype(jnp.int32)
+    movers = jnp.arange(moving, dtype=jnp.int32)
+    moved = jnp.einsum(
+        "jo,orc->jrc",
+        (movers[:, None] + 1 == got_mover[None, :]).astype(jnp.bfloat16),
+        cache_got[:, : cache_used - 1],
+        preferred_element_type=jnp.float32,
+    ).astype(jnp.bfloat16)
+    kv_state = jnp.concatenate([kv_cache[:settled, 0], moved[:, :cache_len]], axis=0)
+    conv_state = jnp.concatenate(
+        [conv_cache[:settled], moved[:, cache_len:].reshape(moving, conv_len, local_width)],
+        axis=0,
+    )
 
     memory = jnp.concatenate([kv_state, fresh], axis=1)
     keys_total = memory.shape[1]
@@ -157,9 +158,11 @@
 
     ctx_all = lax.all_gather(context, "ingest", axis=0, tiled=False)
     row_count = utterances * frame_span
-    attn = grouped_terms(
+    attn = jnp.einsum(
+        "grc,gcn->rn",
         ctx_all.reshape(groups, row_count, head_dim),
         w_out_full.reshape(groups, head_dim, model_width),
+        preferred_element_type=jnp.float32,
     )
     residual = x_rows.reshape(row_count, model_width) + attn
     normed2 = normalize(residual, ln2_gain)
@@ -181,7 +184,12 @@
     activated = jax.nn.silu(running * bn_scale + bn_shift).astype(jnp.bfloat16)
 
     act_all = lax.all_gather(activated, "ingest", axis=0, tiled=False)
-    conv_terms = grouped_terms(act_all.reshape(groups, row_count, local_width), w_pw2_cols)
+    conv_terms = jnp.einsum(
+        "grc,gcn->rn",
+        act_all.reshape(groups, row_count, local_width),
+        w_pw2_cols,
+        preferred_element_type=jnp.float32,
+    )
     residual_own = lax.dynamic_slice_in_dim(residual, me * local_width, local_width, 1)
     result = (residual_own + conv_terms).reshape(utterances, frame_span, local_width)
     live_rows = frame_index[None, :] < frames[:, None]

time: 389 us -> 295 us (0.76)
  waiting for transfers between devices: 238 us -> 185 us
  other arithmetic: 34 us -> 10.4 us
  local copies, waits for them, and re-layouts: 54.9 us -> 32.4 us
  starting transfers between devices: 24.2 us -> 28.6 us
    all_to_all x2, waiting for transfers between devices: 127 us -> 55.4 us  [the longest x1 29.3 us: shards(): lax.all_to_all(frame_send, 'owner', split_axis=0, concat_axis=0, tiled=True)]
    unnamed x70 -> x34, local copies, waits for them, and re-layouts: 36.2 us -> 7.27 us
    all_gather x1 -> x2, waiting for transfers between devices: 32 us -> 55.7 us  [the longest x1 35.4 us: shards(): w_pw2_full = lax.all_gather(w_pw2_in, 'ingest', axis=0, tiled=True)]
    all_gather x1, waiting for transfers between devices: 26.5 us -> 15.1 us  [shards(): x_all = lax.all_gather(arranged, 'ingest', axis=0, tiled=False)]
    all_gather x1, waiting for transfers between devices: 19.9 us -> 29.6 us  [shards(): act_all = lax.all_gather(activated, 'ingest', axis=0, tiled=False)]
    convert_element_type x2 -> x1, other arithmetic: 10.5 us -> 0.84 us  [normalize(): ((values - row_mean) * lax.rsqrt(spread + norm_eps) * gain_cols).astype(j...]
    reduce_sum x2 -> x1, other arithmetic: 8.92 us -> 0.86 us  [normalize(): row_mean = jnp.sum(values, axis=-1, keepdims=True) / model_width]
    all_to_all x2 -> x0, other arithmetic: 7.19 us -> none  [shards(): lax.all_to_all(jnp.concatenate([frame_send, cache_send], axis=1), 'owner'...]
  transfers between devices with their start and end apart: 6 -> 7, of which waited for: 5 -> 7; matrix products, arithmetic and copies ran while one was open for 6% -> 10% of each run, Pallas kernels for 0% -> 0%
where the time goes in v1:
time: 295 us; the launch traced here: 294 us
  waiting for transfers between devices  185 us (63%)
  local copies, waits for them, and re-layouts  32.4 us (11%)
  starting transfers between devices  28.6 us (10%)
  matrix products  22.6 us (8%)
  between operations  14.2 us (5%)
  other arithmetic  10.4 us (4%)
    all_gather x1, waiting for transfers between devices, shards(): w_pw2_full = lax.all_gather(w_pw2_in, 'ingest', axis=0, tiled=True)  35.4 us
    all_gather x1, waiting for transfers between devices, shards(): act_all = lax.all_gather(activated, 'ingest', axis=0, tiled=False)  29.6 us
    all_to_all x1, waiting for transfers between devices, shards(): lax.all_to_all(frame_send, 'owner', split_axis=0, concat_axis=0, tiled=True)  29.3 us
    all_gather x1, waiting for transfers between devices, shards(): ctx_all = lax.all_gather(context, 'ingest', axis=0, tiled=False)  28.9 us
    all_to_all x1, waiting for transfers between devices, shards(): lax.all_to_all(cache_send, 'owner', split_axis=0, concat_axis=0, tiled=True)  26 us
    all_gather x1, waiting for transfers between devices, shards(): w_out_full = lax.all_gather(w_out_in, 'ingest', axis=0, tiled=True)  20.3 us
    all_to_all x1, starting transfers between devices, shards(): lax.all_to_all(frame_send, 'owner', split_axis=0, concat_axis=0, tiled=True)  19.1 us
    all_gather x1, waiting for transfers between devices, shards(): x_all = lax.all_gather(arranged, 'ingest', axis=0, tiled=False)  15.1 us
  transfers between devices with their start and end apart: 7, of which 7 were waited for; matrix products, arithmetic and copies ran while one was open for 10% of the time, Pallas kernels for 0%

profile of v1, /device:TPU:1, one launch (start us, length us, event | category | flops | bytes accessed | tf_op | source)
XLA Modules:
  0.0 293.7 jit_solution(10209997887403494672)
XLA Ops:
  11.4 19.1 %all-to-all-start = ((bf16[64,32,128]{2,1,0:T(8,128)(2,1)}), bf16[64,32,128]{2,1,0:T(8,128)(2,1)S(1)}, u32[]{:S(2)}, u32[]{:S(2)}) async-start(bf16[64,32,128]{2,1,0:T(8,128)(2,1)} %copy.52), calls=%async_computation | async-start | bytes 1048576 | tf_op jit(solution)/shard_map/all_to_all | solution.py:69
  30.6 29.3 %all-to-all-done = bf16[64,32,128]{2,1,0:T(8,128)(2,1)S(1)} async-done(((bf16[64,32,128]{2,1,0:T(8,128)(2,1)}), bf16[64,32,128]{2,1,0:T(8,128)(2,1)S(1)}, u32[]{:S(2)}, u32[]{:S(2)}) %all-to-all-start) | async-done | bytes 524320 | tf_op jit(solution)/shard_map/all_to_all | solution.py:69
  64.0 3.1 %copy.60 = bf16[64,80,256]{2,1,0:T(8,128)(2,1)} copy(bf16[64,80,256]{2,0,1:T(8,128)(2,1)S(1)} %convolution_convert_fusion) | data formatting | bytes 5242880 | tf_op jit(solution)/shard_map/convert_element_type | solution.py:93
  67.1 8.9 %all-to-all-start.1 = ((bf16[64,80,256]{2,1,0:T(8,128)(2,1)}), bf16[64,80,256]{2,1,0:T(8,128)(2,1)}, u32[]{:S(2)}, u32[]{:S(2)}) async-start(bf16[64,80,256]{2,1,0:T(8,128)(2,1)} %copy.60), calls=%async_computation.1 | async-start | bytes 5242880 | tf_op jit(solution)/shard_map/all_to_all | solution.py:94
  76.0 15.1 %all-gather.13.cloned.1.call-done = bf16[264,28,128]{2,1,0:T(8,128)(2,1)} async-done(((bf16[33,28,128]{2,1,0:T(8,128)(2,1)}), bf16[264,28,128]{2,1,0:T(8,128)(2,1)}) %all-gather.13.cloned.1.call-update) | async-done | bytes 1892368 | tf_op jit(solution)/shard_map/all_gather | solution.py:105
  91.1 2.4 copy.69
  97.3 1.6 copy.57
  99.0 4.1 %convert_element_type.199 = bf16[33,28,1024]{2,1,0:T(8,128)(2,1)} reshape(bf16[33,28,8,128]{3,2,1,0:T(8,128)(2,1)} %copy.57) | data formatting | bytes 3784704 | tf_op jit(solution)/shard_map/convert_element_type | solution.py:16
  103.1 2.9 convolution_convert_fusion.1
  106.9 20.3 %all-gather.9.cloned.1.call-done = bf16[1024,1024]{1,0:T(8,128)(2,1)} async-done(((bf16[128,1024]{1,0:T(8,128)(2,1)}), bf16[1024,1024]{1,0:T(8,128)(2,1)}) %all-gather.9.cloned.1.call-update) | async-done | bytes 2097168 | tf_op jit(solution)/shard_map/all_gather | solution.py:107
  127.2 35.4 %all-gather.11.cloned.1.call-done = bf16[1024,1024]{1,0:T(8,128)(2,1)} async-done(((bf16[128,1024]{1,0:T(8,128)(2,1)}), bf16[1024,1024]{1,0:T(8,128)(2,1)}) %all-gather.11.cloned.1.call-update) | async-done | bytes 2097168 | tf_op jit(solution)/shard_map/all_gather | solution.py:108
  163.9 26.0 %all-to-all-done.1 = bf16[64,80,256]{2,1,0:T(8,128)(2,1)} async-done(((bf16[64,80,256]{2,1,0:T(8,128)(2,1)}), bf16[64,80,256]{2,1,0:T(8,128)(2,1)}, u32[]{:S(2)}, u32[]{:S(2)}) %all-to-all-start.1) | async-done | bytes 2621472 | tf_op jit(solution)/shard_map/all_to_all | solution.py:94
  190.0 2.1 fusion.61
  192.1 2.6 fusion.13
  196.5 1.6 fusion.83
  199.1 3.8 %convolution_convert_fusion.4 = bf16[33,28,128]{2,1,0:T(8,128)(2,1)} fusion(bf16[33,98,128]{2,0,1:T(8,128)(2,1)} %get-tuple-element.34, f32[33,28]{1,0:T(8,128)S(1)} %fusion.84, f32[33,28,98]{2,1,0:T(8,128)S(1)} %fusion.27), kind=kOutput, calls=%fused_computation.36 | convolution fusion | flops 23572260 | bytes 1430352 | tf_op jit(solution)/shard_map/sqk,skd->sqd/dot_general | solution.py:155
  204.8 2.8 copy.73
  207.7 28.9 %all-gather.15.cloned.1.call-done = bf16[264,28,128]{2,1,0:T(8,128)(2,1)} async-done(((bf16[33,28,128]{2,1,0:T(8,128)(2,1)}), bf16[264,28,128]{2,1,0:T(8,128)(2,1)}) %all-gather.15.cloned.1.call-update) | async-done | bytes 1892368 | tf_op jit(solution)/shard_map/all_gather | solution.py:159
  236.6 2.5 reshape.341
  239.1 5.1 %fusion.82 = (f32[924]{0:T(1024)S(1)}, f32[924]{0:T(1024)S(1)}, f32[924,1024]{1,0:T(8,128)S(1)}) fusion(f32[924,1024]{1,0:T(8,128)} %bitcast.93, bf16[8,924,128]{2,1,0:T(8,128)(2,1)S(1)} %reshape.341, bf16[8,128,1024]{2,1,0:T(8,128)(2,1)} %bitcast.99), kind=kOutput, calls=%fused_computation.140 | convolution fusion | flops 1941551360 | bytes 11566304 | tf_op jit(solution)/shard_map/grc,gcn->rn/dot_general | solution.py:161
  249.4 2.0 fusion.16
  252.3 29.6 %all-gather.17.cloned.1.call-done = bf16[264,28,128]{2,1,0:T(8,128)(2,1)} async-done(((bf16[33,28,128]{2,1,0:T(8,128)(2,1)}), bf16[264,28,128]{2,1,0:T(8,128)(2,1)}) %all-gather.17.cloned.1.call-update) | async-done | bytes 1892368 | tf_op jit(solution)/shard_map/all_gather | solution.py:186
  281.9 2.5 reshape.346
  284.5 1.7 fusion.28
  (101 shorter events, 25.9 us)
Async XLA Ops:
  7.2 95.9 %copy-start = (bf16[1024,1,384]{2,0,1:T(8,128)(2,1)S(1)}, bf16[1024,1,384]{2,0,1:T(8,128)(2,1)}, u32[]{:S(2)}) copy-start(bf16[1024,1,384]{2,0,1:T(8,128)(2,1)} %param.24) | copy-start | bytes 2359300
  9.1 53.2 %slice-start.2 = ((bf16[33,8,128]{2,1,0:T(8,128)(2,1)}), bf16[32,8,128]{2,1,0:T(8,128)(2,1)S(1)}, s32[]{:S(2)}) async-start(bf16[33,8,128]{2,1,0:T(8,128)(2,1)} %param.21), calls=%async_computation.9 | async-start | bytes 131072 | tf_op jit(solution)/shard_map/slice | solution.py:82
  11.4 48.5 %all-to-all-start = ((bf16[64,32,128]{2,1,0:T(8,128)(2,1)}), bf16[64,32,128]{2,1,0:T(8,128)(2,1)S(1)}, u32[]{:S(2)}, u32[]{:S(2)}) async-start(bf16[64,32,128]{2,1,0:T(8,128)(2,1)} %copy.52), calls=%async_computation | async-start | bytes 1048576 | tf_op jit(solution)/shard_map/all_to_all | solution.py:69
  30.5 31.9 %slice-start.1 = ((bf16[33,1,70,256]{3,2,1,0:T(8,128)(2,1)}), bf16[32,1,70,256]{3,2,1,0:T(8,128)(2,1)S(1)}, s32[]{:S(2)}) async-start(bf16[33,1,70,256]{3,2,1,0:T(8,128)(2,1)} %param.20), calls=%async_computation.8 | async-start | bytes 2359296 | tf_op jit(solution)/shard_map/slice | solution.py:81
  30.5 60.6 %all-gather.13.cloned.1.call-start = ((), (), s32[]{:S(2)}) async-start(), calls=%async_computation.4 | async-start | bytes 2433024 | tf_op jit(solution)/shard_map/all_gather | solution.py:105
  62.4 0.7 copy-start.12
  67.1 122.9 %all-to-all-start.1 = ((bf16[64,80,256]{2,1,0:T(8,128)(2,1)}), bf16[64,80,256]{2,1,0:T(8,128)(2,1)}, u32[]{:S(2)}, u32[]{:S(2)}) async-start(bf16[64,80,256]{2,1,0:T(8,128)(2,1)} %copy.60), calls=%async_computation.1 | async-start | bytes 5242880 | tf_op jit(solution)/shard_map/all_to_all | solution.py:94
  75.9 51.3 %all-gather.9.cloned.1.call-start = ((), (), s32[]{:S(2)}) async-start(), calls=%async_computation.2 | async-start | bytes 2359296 | tf_op jit(solution)/shard_map/all_gather | solution.py:107
  91.1 4.4 %copy-start.8 = (s32[33]{0:T(128)S(1)}, s32[33]{0:T(128)}, u32[]{:S(2)}) copy-start(s32[33]{0:T(128)} %param.19) | copy-start | bytes 400
  93.6 2.9 copy-start.10
  93.6 69.0 %all-gather.11.cloned.1.call-start = ((), (), s32[]{:S(2)}) async-start(), calls=%async_computation.3 | async-start | bytes 2359296 | tf_op jit(solution)/shard_map/all_gather | solution.py:108
  94.3 142.3 %all-gather.15.cloned.1.call-start = ((), (), s32[]{:S(2)}) async-start(), calls=%async_computation.5 | async-start | bytes 2433024 | tf_op jit(solution)/shard_map/all_gather | solution.py:159
  194.7 1.0 copy-start.4
  196.5 2.2 copy-start.2
  198.7 4.5 %copy-start.7 = (bf16[33,8,128]{2,1,0:T(8,128)(2,1)S(1)}, bf16[33,8,128]{2,1,0:T(8,128)(2,1)}, u32[]{:S(2)}) copy-start(bf16[33,8,128]{2,1,0:T(8,128)(2,1)} %param.21) | copy-start | bytes 202756
  198.7 4.5 %copy-start.9 = (bf16[9,128]{1,0:T(8,128)(2,1)S(1)}, bf16[9,128]{1,0:T(8,128)(2,1)}, u32[]{:S(2)}) copy-start(bf16[9,128]{1,0:T(8,128)(2,1)} %param.28) | copy-start | bytes 6916
  202.9 79.0 %all-gather.17.cloned.1.call-start = ((), (), s32[]{:S(2)}) async-start(), calls=%async_computation.6 | async-start | bytes 2433024 | tf_op jit(solution)/shard_map/all_gather | solution.py:186
  204.8 2.8 slice-start
  239.1 5.2 %copy-start.6 = (bf16[1024,2,128]{2,1,0:T(2,128)(2,1)S(1)}, bf16[1024,2,128]{2,1,0:T(2,128)(2,1)}, u32[]{:S(2)}) copy-start(bf16[1024,2,128]{2,1,0:T(2,128)(2,1)} %param.27) | copy-start | bytes 1572868
  239.1 5.2 %copy-start.11 = (f32[1024]{0:T(1024)S(1)}, f32[1024]{0:T(1024)}, u32[]{:S(2)}) copy-start(f32[1024]{0:T(1024)} %param.26) | copy-start | bytes 12292
  244.2 1.9 copy-start.5
  246.1 0.7 copy-start.14
  246.8 2.6 copy-start.3
  281.9 5.2 %copy-start.1 = (bf16[1024,1,384]{2,0,1:T(8,128)(2,1)S(1)}, bf16[1024,1,384]{2,0,1:T(8,128)(2,1)}, u32[]{:S(2)}) copy-start(bf16[1024,1,384]{2,0,1:T(8,128)(2,1)} %param.24) | copy-start | bytes 2359300
  (1 other events, 0.7 us)
Sparse Core Ops, SparseCore 0:
  62.3 28.7 all-gather.12
  93.7 33.4 all-gather.8
  129.4 33.2 all-gather.10
  203.1 33.4 all-gather.14
  248.3 33.5 all-gather.16

commit v2 on v1

--- a/solution.py
+++ b/solution.py
@@ -66,7 +66,6 @@
         frame_rows_tagged,
         preferred_element_type=jnp.float32,
     ).astype(jnp.bfloat16)
-    frame_got = lax.all_to_all(frame_send, "owner", split_axis=0, concat_axis=0, tiled=True)
 
     kv_lanes = 2 * head_dim
     conv_fold = conv_len * local_width // kv_lanes
@@ -91,16 +90,14 @@
         cache_rows,
         preferred_element_type=jnp.float32,
     ).astype(jnp.bfloat16)
+    frame_send, cache_send = lax.optimization_barrier((frame_send, cache_send))
+    frame_got = lax.all_to_all(frame_send, "owner", split_axis=0, concat_axis=0, tiled=True)
     cache_got = lax.all_to_all(cache_send, "owner", split_axis=0, concat_axis=0, tiled=True)
 
     got_slot = frame_got[:, frame_span, 0].astype(jnp.int32)
     slots = jnp.arange(utterances, dtype=jnp.int32)
-    arranged = jnp.einsum(
-        "so,otc->stc",
-        (slots[:, None] + 1 == got_slot[None, :]).astype(jnp.bfloat16),
-        frame_got[:, :frame_span],
-        preferred_element_type=jnp.float32,
-    ).astype(jnp.bfloat16)
+    frame_from = jnp.argmax(slots[:, None] + 1 == got_slot[None, :], axis=1)
+    arranged = frame_got[frame_from, :frame_span]
 
     x_all = lax.all_gather(arranged, "ingest", axis=0, tiled=False)
     w_out_in, w_pw2_in, x_all = lax.optimization_barrier((w_out, w_pw2, x_all))
@@ -123,12 +120,8 @@
 
     got_mover = cache_got[:, cache_used - 1, 0].astype(jnp.int32)
     movers = jnp.arange(moving, dtype=jnp.int32)
-    moved = jnp.einsum(
-        "jo,orc->jrc",
-        (movers[:, None] + 1 == got_mover[None, :]).astype(jnp.bfloat16),
-        cache_got[:, : cache_used - 1],
-        preferred_element_type=jnp.float32,
-    ).astype(jnp.bfloat16)
+    cache_from = jnp.argmax(movers[:, None] + 1 == got_mover[None, :], axis=1)
+    moved = cache_got[cache_from, : cache_used - 1]
     kv_state = jnp.concatenate([kv_cache[:settled, 0], moved[:, :cache_len]], axis=0)
     conv_state = jnp.concatenate(
         [conv_cache[:settled], moved[:, cache_len:].reshape(moving, conv_len, local_width)],

time: 295 us -> 307 us (1.041)
  local copies, waits for them, and re-layouts: 32.4 us -> 43.9 us
  waiting for transfers between devices: 185 us -> 189 us
  matrix products: 22.6 us -> 19.1 us
    gather x0 -> x3, local copies, waits for them, and re-layouts: none -> 8.39 us  [the longest x1 5.09 us: shards(): moved = cache_got[cache_from, :cache_used - 1]]
    convert_element_type x3 -> x0, local copies, waits for them, and re-layouts: 4.95 us -> none  [the longest x1 3.07 us: shards(): cache_send = jnp.einsum('dj,jrc->drc', (dest[:, None] == mig_owner[None,...]
    optimization_barrier x1 -> x2, local copies, waits for them, and re-layouts: 1.31 us -> 5.9 us  [shards(): frame_send, cache_send = lax.optimization_barrier((frame_send, cache_send))]
    all_gather x1, waiting for transfers between devices: 20.3 us -> 23.5 us  [shards(): w_out_full = lax.all_gather(w_out_in, 'ingest', axis=0, tiled=True)]
    unnamed x34 -> x45, local copies, waits for them, and re-layouts: 7.27 us -> 8.23 us
  transfers between devices with their start and end apart: 7 -> 7, of which waited for: 7 -> 7; matrix products, arithmetic and copies ran while one was open for 10% -> 8% of each run, Pallas kernels for 0% -> 0%
where the time goes in v2:
time: 307 us; the launch traced here: 306 us
  waiting for transfers between devices  189 us (62%)
  local copies, waits for them, and re-layouts  43.9 us (14%)
  starting transfers between devices  28.4 us (9%)
  matrix products  19.1 us (6%)
  between operations  14.3 us (5%)
  other arithmetic  11.4 us (4%)
    all_gather x1, waiting for transfers between devices, shards(): w_pw2_full = lax.all_gather(w_pw2_in, 'ingest', axis=0, tiled=True)  35.4 us
    all_gather x1, waiting for transfers between devices, shards(): act_all = lax.all_gather(activated, 'ingest', axis=0, tiled=False)  29.6 us
    all_to_all x1, waiting for transfers between devices, shards(): lax.all_to_all(frame_send, 'owner', split_axis=0, concat_axis=0, tiled=True)  29.3 us
    all_gather x1, waiting for transfers between devices, shards(): ctx_all = lax.all_gather(context, 'ingest', axis=0, tiled=False)  28.2 us
    all_to_all x1, waiting for transfers between devices, shards(): lax.all_to_all(cache_send, 'owner', split_axis=0, concat_axis=0, tiled=True)  27.2 us
    all_gather x1, waiting for transfers between devices, shards(): w_out_full = lax.all_gather(w_out_in, 'ingest', axis=0, tiled=True)  23.5 us
    all_to_all x1, starting transfers between devices, shards(): lax.all_to_all(frame_send, 'owner', split_axis=0, concat_axis=0, tiled=True)  19.1 us
    all_gather x1, waiting for transfers between devices, shards(): x_all = lax.all_gather(arranged, 'ingest', axis=0, tiled=False)  15.2 us
  transfers between devices with their start and end apart: 7, of which 7 were waited for; matrix products, arithmetic and copies ran while one was open for 8% of the time, Pallas kernels for 0%

profile of v2, /device:TPU:1, one launch (start us, length us, event | category | flops | bytes accessed | tf_op | source)
XLA Modules:
  0.0 306.4 jit_solution(16158593876140652399)
XLA Ops:
  11.3 2.4 convolution_convert_fusion
  14.9 19.1 %all-to-all-start = ((bf16[64,32,128]{2,1,0:T(8,128)(2,1)}), bf16[64,32,128]{2,1,0:T(8,128)(2,1)S(1)}, u32[]{:S(2)}, u32[]{:S(2)}) async-start(bf16[64,32,128]{2,1,0:T(8,128)(2,1)} %copy.57), calls=%async_computation | async-start | bytes 1048576 | tf_op jit(solution)/shard_map/all_to_all | solution.py:94
  34.1 29.3 %all-to-all-done = bf16[64,32,128]{2,1,0:T(8,128)(2,1)S(1)} async-done(((bf16[64,32,128]{2,1,0:T(8,128)(2,1)}), bf16[64,32,128]{2,1,0:T(8,128)(2,1)S(1)}, u32[]{:S(2)}, u32[]{:S(2)}) %all-to-all-start) | async-done | bytes 524320 | tf_op jit(solution)/shard_map/all_to_all | solution.py:94
  65.5 2.5 gather_fusion
  68.9 4.8 %copy.63 = bf16[64,80,256]{2,1,0:T(8,128)(2,1)} copy(bf16[64,80,256]{2,0,1:T(8,128)(2,1)} %convolution_convert_fusion) | data formatting | bytes 5242880 | tf_op jit(solution)/shard_map/optimization_barrier | solution.py:93
  73.6 8.9 %all-to-all-start.1 = ((bf16[64,80,256]{2,1,0:T(8,128)(2,1)}), bf16[64,80,256]{2,1,0:T(8,128)(2,1)}, u32[]{:S(2)}, u32[]{:S(2)}) async-start(bf16[64,80,256]{2,1,0:T(8,128)(2,1)} %copy.63), calls=%async_computation.1 | async-start | bytes 5242880 | tf_op jit(solution)/shard_map/all_to_all | solution.py:95
  82.6 15.2 %all-gather.13.cloned.1.call-done = bf16[264,28,128]{2,1,0:T(8,128)(2,1)} async-done(((bf16[33,28,128]{2,1,0:T(8,128)(2,1)}), bf16[264,28,128]{2,1,0:T(8,128)(2,1)}) %all-gather.13.cloned.1.call-update) | async-done | bytes 1892368 | tf_op jit(solution)/shard_map/all_gather | solution.py:102
  97.8 2.4 copy.68
  105.3 2.9 convert_element_type.192
  110.4 23.5 %all-gather.9.cloned.1.call-done = bf16[1024,1024]{1,0:T(8,128)(2,1)} async-done(((bf16[128,1024]{1,0:T(8,128)(2,1)}), bf16[1024,1024]{1,0:T(8,128)(2,1)}) %all-gather.9.cloned.1.call-update) | async-done | bytes 2097168 | tf_op jit(solution)/shard_map/all_gather | solution.py:104
  133.9 35.4 %all-gather.11.cloned.1.call-done = bf16[1024,1024]{1,0:T(8,128)(2,1)} async-done(((bf16[128,1024]{1,0:T(8,128)(2,1)}), bf16[1024,1024]{1,0:T(8,128)(2,1)}) %all-gather.11.cloned.1.call-update) | async-done | bytes 2097168 | tf_op jit(solution)/shard_map/all_gather | solution.py:105
  169.3 27.2 %all-to-all-done.1 = bf16[64,80,256]{2,1,0:T(8,128)(2,1)} async-done(((bf16[64,80,256]{2,1,0:T(8,128)(2,1)}), bf16[64,80,256]{2,1,0:T(8,128)(2,1)}, u32[]{:S(2)}, u32[]{:S(2)}) %all-to-all-start.1) | async-done | bytes 2621472 | tf_op jit(solution)/shard_map/all_to_all | solution.py:95
  196.6 2.1 fusion.48
  199.4 2.6 copy.64
  202.0 5.1 %gather_fusion.1 = bf16[32,74,256]{2,0,1:T(8,128)(2,1)} fusion(bf16[64,80,256]{2,0,1:T(8,128)(2,1)S(1)} %copy.64, s32[32]{0:T(128)S(1)} %fusion.59), kind=kCustom, calls=%fused_computation.1 | custom fusion | bytes 2425088 | tf_op jit(solution)/shard_map/gather | solution.py:124
  211.7 4.0 %convolution_convert_fusion.4 = bf16[33,28,128]{2,1,0:T(8,128)(2,1)} fusion(bf16[33,98,256]{2,1,0:T(8,128)(2,1)} %copy-done.9, f32[33,28]{1,0:T(8,128)S(1)} %fusion.66, f32[33,28,98]{2,1,0:T(8,128)S(1)} %fusion.15), kind=kOutput, calls=%fused_computation.32 | convolution fusion | flops 23572260 | bytes 2216960 | tf_op jit(solution)/shard_map/sqk,skd->sqd/dot_general | solution.py:148
  218.2 2.8 copy.71
  221.1 28.2 %all-gather.15.cloned.1.call-done = bf16[264,28,128]{2,1,0:T(8,128)(2,1)} async-done(((bf16[33,28,128]{2,1,0:T(8,128)(2,1)}), bf16[264,28,128]{2,1,0:T(8,128)(2,1)}) %all-gather.15.cloned.1.call-update) | async-done | bytes 1892368 | tf_op jit(solution)/shard_map/all_gather | solution.py:152
  249.3 2.5 reshape.341
  251.8 5.1 %fusion.65 = (f32[924]{0:T(1024)S(1)}, f32[924]{0:T(1024)S(1)}, f32[924,1024]{1,0:T(8,128)S(1)}) fusion(f32[924,1024]{1,0:T(8,128)} %bitcast.85, bf16[8,924,128]{2,1,0:T(8,128)(2,1)S(1)} %reshape.341, bf16[8,128,1024]{2,1,0:T(8,128)(2,1)} %bitcast.90), kind=kOutput, calls=%fused_computation.135 | convolution fusion | flops 1941551360 | bytes 11566304 | tf_op jit(solution)/shard_map/grc,gcn->rn/dot_general | solution.py:154
  262.2 1.9 fusion.6
  265.1 29.6 %all-gather.17.cloned.1.call-done = bf16[264,28,128]{2,1,0:T(8,128)(2,1)} async-done(((bf16[33,28,128]{2,1,0:T(8,128)(2,1)}), bf16[264,28,128]{2,1,0:T(8,128)(2,1)}) %all-gather.17.cloned.1.call-update) | async-done | bytes 1892368 | tf_op jit(solution)/shard_map/all_gather | solution.py:179
  294.7 2.5 reshape.346
  297.2 1.7 fusion.16
  (115 shorter events, 30.1 us)
Async XLA Ops:
  7.2 101.1 %copy-start = (bf16[1024,1,384]{2,0,1:T(8,128)(2,1)S(1)}, bf16[1024,1,384]{2,0,1:T(8,128)(2,1)}, u32[]{:S(2)}) copy-start(bf16[1024,1,384]{2,0,1:T(8,128)(2,1)} %param.24) | copy-start | bytes 2359300
  7.2 3.0 slice-start.2
  14.9 48.5 %all-to-all-start = ((bf16[64,32,128]{2,1,0:T(8,128)(2,1)}), bf16[64,32,128]{2,1,0:T(8,128)(2,1)S(1)}, u32[]{:S(2)}, u32[]{:S(2)}) async-start(bf16[64,32,128]{2,1,0:T(8,128)(2,1)} %copy.57), calls=%async_computation | async-start | bytes 1048576 | tf_op jit(solution)/shard_map/all_to_all | solution.py:94
  34.0 63.8 %all-gather.13.cloned.1.call-start = ((), (), s32[]{:S(2)}) async-start(), calls=%async_computation.4 | async-start | bytes 2433024 | tf_op jit(solution)/shard_map/all_gather | solution.py:102
  73.6 122.9 %all-to-all-start.1 = ((bf16[64,80,256]{2,1,0:T(8,128)(2,1)}), bf16[64,80,256]{2,1,0:T(8,128)(2,1)}, u32[]{:S(2)}, u32[]{:S(2)}) async-start(bf16[64,80,256]{2,1,0:T(8,128)(2,1)} %copy.63), calls=%async_computation.1 | async-start | bytes 5242880 | tf_op jit(solution)/shard_map/all_to_all | solution.py:95
  82.5 51.4 %all-gather.9.cloned.1.call-start = ((), (), s32[]{:S(2)}) async-start(), calls=%async_computation.2 | async-start | bytes 2359296 | tf_op jit(solution)/shard_map/all_gather | solution.py:104
  97.8 3.4 %copy-start.12 = (s32[33]{0:T(128)S(1)}, s32[33]{0:T(128)}, u32[]{:S(2)}) copy-start(s32[33]{0:T(128)} %param.19) | copy-start | bytes 400
  100.2 3.5 %copy-start.2 = (bf16[8,33,28,128]{3,1,0,2:T(8,128)(2,1)}, bf16[8,33,28,128]{3,1,0,2:T(8,128)(2,1)S(1)}, u32[]{:S(2)}) copy-start(bf16[8,33,28,128]{3,1,0,2:T(8,128)(2,1)S(1)} %copy.68) | copy-start | bytes 5677060
  100.2 2.7 copy-start.14
  100.3 69.1 %all-gather.11.cloned.1.call-start = ((), (), s32[]{:S(2)}) async-start(), calls=%async_computation.3 | async-start | bytes 2359296 | tf_op jit(solution)/shard_map/all_gather | solution.py:105
  101.0 148.3 %all-gather.15.cloned.1.call-start = ((), (), s32[]{:S(2)}) async-start(), calls=%async_computation.5 | async-start | bytes 2433024 | tf_op jit(solution)/shard_map/all_gather | solution.py:152
  110.4 98.7 %copy-start.7 = (bf16[33,28,256]{2,1,0:T(8,128)(2,1)}, bf16[33,28,256]{2,1,0:T(8,128)(2,1)S(1)}, u32[]{:S(2)}) copy-start(bf16[33,28,256]{2,1,0:T(8,128)(2,1)S(1)} %slice.136) | copy-start | bytes 1419268
  209.1 2.3 copy-start.5
  209.1 1.7 copy-start.11
  211.3 5.3 %copy-start.13 = (bf16[9,128]{1,0:T(8,128)(2,1)S(1)}, bf16[9,128]{1,0:T(8,128)(2,1)}, u32[]{:S(2)}) copy-start(bf16[9,128]{1,0:T(8,128)(2,1)} %param.28) | copy-start | bytes 6916
  211.3 5.3 %copy-start.3 = (bf16[8,33,28,128]{3,1,0,2:T(8,128)(2,1)S(1)}, bf16[8,33,28,128]{3,1,0,2:T(8,128)(2,1)}, u32[]{:S(2)}) copy-start(bf16[8,33,28,128]{3,1,0,2:T(8,128)(2,1)} %copy-done.2) | copy-start | bytes 5677060
  215.7 79.0 %all-gather.17.cloned.1.call-start = ((), (), s32[]{:S(2)}) async-start(), calls=%async_computation.6 | async-start | bytes 2433024 | tf_op jit(solution)/shard_map/all_gather | solution.py:179
  218.2 2.8 slice-start.1
  251.8 5.2 %copy-start.10 = (bf16[1024,2,128]{2,1,0:T(2,128)(2,1)S(1)}, bf16[1024,2,128]{2,1,0:T(2,128)(2,1)}, u32[]{:S(2)}) copy-start(bf16[1024,2,128]{2,1,0:T(2,128)(2,1)} %param.27) | copy-start | bytes 1572868
  251.8 5.2 %copy-start.15 = (f32[1024]{0:T(1024)S(1)}, f32[1024]{0:T(1024)}, u32[]{:S(2)}) copy-start(f32[1024]{0:T(1024)} %param.26) | copy-start | bytes 12292
  256.9 1.9 copy-start.4
  259.5 2.6 copy-start.6
  259.5 2.7 copy-start.8
  294.7 5.2 %copy-start.1 = (bf16[1024,1,384]{2,0,1:T(8,128)(2,1)S(1)}, bf16[1024,1,384]{2,0,1:T(8,128)(2,1)}, u32[]{:S(2)}) copy-start(bf16[1024,1,384]{2,0,1:T(8,128)(2,1)} %param.24) | copy-start | bytes 2359300
  (6 other events, 5.7 us)
Sparse Core Ops, SparseCore 0:
  69.0 28.7 all-gather.12
  100.4 33.4 all-gather.8
  136.1 33.2 all-gather.10
  215.8 33.4 all-gather.14
  261.1 33.5 all-gather.16

commit v3 on v1

--- a/solution.py
+++ b/solution.py
@@ -4,6 +4,7 @@
 from jax.sharding import PartitionSpec as P
 
 BLOCKS = 2
+CHUNK_MIN = 19
 
 
 norm_eps = 1e-05
@@ -135,6 +136,31 @@
         axis=0,
     )
 
+    split = (utterances + 1) // 2
+    chunk = max(split, CHUNK_MIN)
+    pieces = []
+    for lo, hi in ((0, split), (split, utterances)):
+        extra = chunk - (hi - lo)
+        grow = lambda a: jnp.pad(a[lo:hi], ((0, extra),) + ((0, 0),) * (a.ndim - 1))
+        outs = chunk_layer(
+            grow(queries), grow(fresh), grow(kv_state), grow(conv_state), grow(x_rows),
+            grow(frames), w_out_full, w_pw1, w_pw2_cols, dw_weight, bn_scale, bn_shift,
+            ln2_gain, me, groups, horizon,
+        )
+        pieces.append(tuple(o[: hi - lo] for o in outs))
+    return tuple(jnp.concatenate(parts, axis=0) for parts in zip(*pieces))
+
+
+def chunk_layer(
+    queries, fresh, kv_state, conv_state, x_rows, frames, w_out_full, w_pw1, w_pw2_cols,
+    dw_weight, bn_scale, bn_shift, ln2_gain, me, groups, horizon,
+):
+    utterances, frame_span, model_width = x_rows.shape
+    head_dim = queries.shape[-1]
+    cache_len = kv_state.shape[1]
+    conv_len = conv_state.shape[1]
+    local_width = conv_state.shape[2]
+    taps = dw_weight.shape[0]
     memory = jnp.concatenate([kv_state, fresh], axis=1)
     keys_total = memory.shape[1]
     scores = jnp.einsum(
@@ -206,7 +232,7 @@
     conv_next = jnp.einsum(
         "srp,spd->srd", conv_pick.astype(jnp.bfloat16), joined, preferred_element_type=jnp.float32
     ).astype(jnp.bfloat16)
-    return (layer_out, kv_next.reshape(kv_cache.shape), conv_next)
+    return (layer_out, kv_next[:, None], conv_next)
 
 
 def solution(mesh):

time: 295 us -> 346 us (1.17)
  waiting for transfers between devices: 185 us -> 213 us
  local copies, waits for them, and re-layouts: 32.4 us -> 45.4 us
  other arithmetic: 10.4 us -> 16.3 us
  matrix products: 22.6 us -> 27 us
    all_gather x2 -> x4, waiting for transfers between devices: 58.5 us -> 84.9 us  [the longest x2 53.7 us: chunk_layer(): act_all = lax.all_gather(activated, 'ingest', axis=0, tiled=False)]
    reshape x4 -> x10, local copies, waits for them, and re-layouts: 5.1 us -> 11 us  [the longest x2 4.51 us: chunk_layer(): residual = x_rows.reshape(row_count, model_width) + attn]
    another operation x0 -> x3, local copies, waits for them, and re-layouts: none -> 4.39 us
    dot_general x7 -> x14, matrix products: 14.8 us -> 19.2 us  [the longest x2 7.26 us: chunk_layer(): jnp.einsum('grc,gcn->rn', ctx_all.reshape(groups, row_count, head_dim), w...]
    unnamed x34 -> x55, local copies, waits for them, and re-layouts: 7.27 us -> 8.21 us
  transfers between devices with their start and end apart: 7 -> 9, of which waited for: 7 -> 9; matrix products, arithmetic and copies ran while one was open for 10% -> 18% of each run, Pallas kernels for 0% -> 0%
where the time goes in v3:
time: 346 us; the launch traced here: 345 us
  waiting for transfers between devices  213 us (62%)
  local copies, waits for them, and re-layouts  45.4 us (13%)
  starting transfers between devices  28.7 us (8%)
  matrix products  27 us (8%)
  other arithmetic  16.3 us (5%)
  between operations  14.9 us (4%)
    all_gather x2, waiting for transfers between devices, chunk_layer(): act_all = lax.all_gather(activated, 'ingest', axis=0, tiled=False)  53.7 us
    all_gather x1, waiting for transfers between devices, shards(): w_pw2_full = lax.all_gather(w_pw2_in, 'ingest', axis=0, tiled=True)  35.4 us
    all_gather x2, waiting for transfers between devices, chunk_layer(): ctx_all = lax.all_gather(context, 'ingest', axis=0, tiled=False)  31.2 us
    all_to_all x1, waiting for transfers between devices, shards(): lax.all_to_all(frame_send, 'owner', split_axis=0, concat_axis=0, tiled=True)  29.3 us
    all_to_all x1, waiting for transfers between devices, shards(): lax.all_to_all(cache_send, 'owner', split_axis=0, concat_axis=0, tiled=True)  27.2 us
    all_gather x1, waiting for transfers between devices, shards(): w_out_full = lax.all_gather(w_out_in, 'ingest', axis=0, tiled=True)  20.1 us
    all_to_all x1, starting transfers between devices, shards(): lax.all_to_all(frame_send, 'owner', split_axis=0, concat_axis=0, tiled=True)  19.1 us
    all_gather x1, waiting for transfers between devices, shards(): x_all = lax.all_gather(arranged, 'ingest', axis=0, tiled=False)  15.1 us
  transfers between devices with their start and end apart: 9, of which 9 were waited for; matrix products, arithmetic and copies ran while one was open for 18% of the time, Pallas kernels for 0%

profile of v3, /device:TPU:1, one launch (start us, length us, event | category | flops | bytes accessed | tf_op | source)
XLA Modules:
  0.0 345.1 jit_solution(12299032184313702296)
XLA Ops:
  11.4 19.1 %all-to-all-start = ((bf16[64,32,128]{2,1,0:T(8,128)(2,1)}), bf16[64,32,128]{2,1,0:T(8,128)(2,1)S(1)}, u32[]{:S(2)}, u32[]{:S(2)}) async-start(bf16[64,32,128]{2,1,0:T(8,128)(2,1)} %copy.69), calls=%async_computation | async-start | bytes 1048576 | tf_op jit(solution)/shard_map/all_to_all | solution.py:70
  30.6 29.3 %all-to-all-done = bf16[64,32,128]{2,1,0:T(8,128)(2,1)S(1)} async-done(((bf16[64,32,128]{2,1,0:T(8,128)(2,1)}), bf16[64,32,128]{2,1,0:T(8,128)(2,1)S(1)}, u32[]{:S(2)}, u32[]{:S(2)}) %all-to-all-start) | async-done | bytes 524320 | tf_op jit(solution)/shard_map/all_to_all | solution.py:70
  64.0 3.0 copy.77
  67.0 8.9 %all-to-all-start.1 = ((bf16[64,80,256]{2,1,0:T(8,128)(2,1)}), bf16[64,80,256]{2,1,0:T(8,128)(2,1)}, u32[]{:S(2)}, u32[]{:S(2)}) async-start(bf16[64,80,256]{2,1,0:T(8,128)(2,1)} %copy.77), calls=%async_computation.1 | async-start | bytes 5242880 | tf_op jit(solution)/shard_map/all_to_all | solution.py:95
  76.0 15.1 %all-gather.17.cloned.1.call-done = bf16[264,28,128]{2,1,0:T(8,128)(2,1)} async-done(((bf16[33,28,128]{2,1,0:T(8,128)(2,1)}), bf16[264,28,128]{2,1,0:T(8,128)(2,1)}) %all-gather.17.cloned.1.call-update) | async-done | bytes 1892368 | tf_op jit(solution)/shard_map/all_gather | solution.py:106
  91.1 2.5 copy.93
  99.3 4.1 %convert_element_type.250 = bf16[33,28,1024]{2,1,0:T(8,128)(2,1)} reshape(bf16[33,28,8,128]{3,2,1,0:T(8,128)(2,1)} %copy.74) | data formatting | bytes 3784704 | tf_op jit(solution)/shard_map/convert_element_type | solution.py:17
  103.4 2.9 convolution_convert_fusion.1
  107.1 20.1 %all-gather.13.cloned.1.call-done = bf16[1024,1024]{1,0:T(8,128)(2,1)} async-done(((bf16[128,1024]{1,0:T(8,128)(2,1)}), bf16[1024,1024]{1,0:T(8,128)(2,1)}) %all-gather.13.cloned.1.call-update) | async-done | bytes 2097168 | tf_op jit(solution)/shard_map/all_gather | solution.py:108
  127.2 35.4 %all-gather.15.cloned.1.call-done = bf16[1024,1024]{1,0:T(8,128)(2,1)} async-done(((bf16[128,1024]{1,0:T(8,128)(2,1)}), bf16[1024,1024]{1,0:T(8,128)(2,1)}) %all-gather.15.cloned.1.call-update) | async-done | bytes 2097168 | tf_op jit(solution)/shard_map/all_gather | solution.py:109
  162.8 27.2 %all-to-all-done.1 = bf16[64,80,256]{2,1,0:T(8,128)(2,1)} async-done(((bf16[64,80,256]{2,1,0:T(8,128)(2,1)}), bf16[64,80,256]{2,1,0:T(8,128)(2,1)}, u32[]{:S(2)}, u32[]{:S(2)}) %all-to-all-start.1) | async-done | bytes 2621472 | tf_op jit(solution)/shard_map/all_to_all | solution.py:95
  190.0 2.1 fusion.111
  192.1 2.6 fusion.7
  197.6 2.8 convolution_convert_fusion.4
  205.8 2.4 reshape.477
  212.7 2.8 convolution_convert_fusion.5
  217.6 2.9 reshape.478
  224.9 7.8 %all-gather.23.cloned.1.call-done = bf16[152,28,128]{2,1,0:T(8,128)(2,1)} async-done(((bf16[19,28,128]{2,1,0:T(8,128)(2,1)}), bf16[152,28,128]{2,1,0:T(8,128)(2,1)}) %all-gather.23.cloned.1.call-update) | async-done | bytes 1089552 | tf_op jit(solution)/shard_map/all_gather | solution.py:185
  232.7 2.2 reshape.490
  234.9 3.5 %fusion.138 = (f32[532]{0:T(1024)S(1)}, f32[532]{0:T(1024)S(1)}, f32[532,1024]{1,0:T(8,128)S(1)}) fusion(f32[532,1024]{1,0:T(8,128)S(1)} %copy-done.11, bf16[8,532,128]{2,1,0:T(8,128)(2,1)} %reshape.490, bf16[8,128,1024]{2,1,0:T(8,128)(2,1)} %bitcast.115), kind=kOutput, calls=%fused_computation.245 | convolution fusion | flops 1117862912 | bytes 7549088 | tf_op jit(solution)/shard_map/grc,gcn->rn/dot_general | solution.py:187
  243.0 23.3 %all-gather.19.cloned.1.call-done = bf16[152,28,128]{2,1,0:T(8,128)(2,1)} async-done(((bf16[19,28,128]{2,1,0:T(8,128)(2,1)}), bf16[152,28,128]{2,1,0:T(8,128)(2,1)}) %all-gather.19.cloned.1.call-update) | async-done | bytes 1089552 | tf_op jit(solution)/shard_map/all_gather | solution.py:185
  267.7 3.8 %fusion.137 = (f32[532]{0:T(1024)S(1)}, f32[532]{0:T(1024)S(1)}, f32[532,1024]{1,0:T(8,128)S(1)}) fusion(f32[532,1024]{1,0:T(8,128)} %reshape.478, bf16[8,532,128]{2,1,0:T(8,128)(2,1)S(1)} %reshape.481, bf16[8,128,1024]{2,1,0:T(8,128)(2,1)} %bitcast.116), kind=kOutput, calls=%fused_computation.244 | convolution fusion | flops 1117862912 | bytes 7549088 | tf_op jit(solution)/shard_map/grc,gcn->rn/dot_general | solution.py:187
  277.7 22.8 %all-gather.25.cloned.1.call-done = bf16[152,28,128]{2,1,0:T(8,128)(2,1)} async-done(((bf16[19,28,128]{2,1,0:T(8,128)(2,1)}), bf16[152,28,128]{2,1,0:T(8,128)(2,1)}) %all-gather.25.cloned.1.call-update) | async-done | bytes 1089552 | tf_op jit(solution)/shard_map/all_gather | solution.py:212
  303.4 30.9 %all-gather.21.cloned.1.call-done = bf16[152,28,128]{2,1,0:T(8,128)(2,1)} async-done(((bf16[19,28,128]{2,1,0:T(8,128)(2,1)}), bf16[152,28,128]{2,1,0:T(8,128)(2,1)}) %all-gather.21.cloned.1.call-update) | async-done | bytes 1089552 | tf_op jit(solution)/shard_map/all_gather | solution.py:212
  (180 shorter events, 52.6 us)
Async XLA Ops:
  7.2 96.2 %copy-start = (bf16[1024,1,384]{2,0,1:T(8,128)(2,1)S(1)}, bf16[1024,1,384]{2,0,1:T(8,128)(2,1)}, u32[]{:S(2)}) copy-start(bf16[1024,1,384]{2,0,1:T(8,128)(2,1)} %param.24) | copy-start | bytes 2359300
  9.1 53.2 %slice-start.3 = ((bf16[33,8,128]{2,1,0:T(8,128)(2,1)}), bf16[32,8,128]{2,1,0:T(8,128)(2,1)S(1)}, s32[]{:S(2)}) async-start(bf16[33,8,128]{2,1,0:T(8,128)(2,1)} %param.21), calls=%async_computation.12 | async-start | bytes 131072 | tf_op jit(solution)/shard_map/slice | solution.py:83
  11.4 48.5 %all-to-all-start = ((bf16[64,32,128]{2,1,0:T(8,128)(2,1)}), bf16[64,32,128]{2,1,0:T(8,128)(2,1)S(1)}, u32[]{:S(2)}, u32[]{:S(2)}) async-start(bf16[64,32,128]{2,1,0:T(8,128)(2,1)} %copy.69), calls=%async_computation | async-start | bytes 1048576 | tf_op jit(solution)/shard_map/all_to_all | solution.py:70
  30.5 60.6 %all-gather.17.cloned.1.call-start = ((), (), s32[]{:S(2)}) async-start(), calls=%async_computation.4 | async-start | bytes 2433024 | tf_op jit(solution)/shard_map/all_gather | solution.py:106
  67.0 122.9 %all-to-all-start.1 = ((bf16[64,80,256]{2,1,0:T(8,128)(2,1)}), bf16[64,80,256]{2,1,0:T(8,128)(2,1)}, u32[]{:S(2)}, u32[]{:S(2)}) async-start(bf16[64,80,256]{2,1,0:T(8,128)(2,1)} %copy.77), calls=%async_computation.1 | async-start | bytes 5242880 | tf_op jit(solution)/shard_map/all_to_all | solution.py:95
  75.9 51.3 %all-gather.13.cloned.1.call-start = ((), (), s32[]{:S(2)}) async-start(), calls=%async_computation.2 | async-start | bytes 2359296 | tf_op jit(solution)/shard_map/all_gather | solution.py:108
  91.1 3.5 %copy-start.24 = (s32[33]{0:T(128)S(1)}, s32[33]{0:T(128)}, u32[]{:S(2)}) copy-start(s32[33]{0:T(128)} %param.19) | copy-start | bytes 400
  91.1 3.6 %copy-start.18 = (pred[19]{0:T(512)(128)(4,1)S(1)}, pred[19]{0:T(512)(128)(4,1)}, u32[]{:S(2)}) copy-start(pred[19]{0:T(512)(128)(4,1)} %constant.24.clone.1) | copy-start | bytes 61
  91.1 3.8 %copy-start.19 = (bf16[9,128]{1,0:T(8,128)(2,1)S(1)}, bf16[9,128]{1,0:T(8,128)(2,1)}, u32[]{:S(2)}) copy-start(bf16[9,128]{1,0:T(8,128)(2,1)} %param.28) | copy-start | bytes 6916
  93.6 3.3 copy-start.20
  93.6 69.0 %all-gather.15.cloned.1.call-start = ((), (), s32[]{:S(2)}) async-start(), calls=%async_computation.3 | async-start | bytes 2359296 | tf_op jit(solution)/shard_map/all_gather | solution.py:109
  94.4 138.4 %all-gather.23.cloned.1.call-start = ((), (), s32[]{:S(2)}) async-start(), calls=%async_computation.7 | async-start | bytes 1400832 | tf_op jit(solution)/shard_map/all_gather | solution.py:185
  94.8 105.7 %copy-start.17 = (pred[19,28]{1,0:T(8,128)(4,1)}, pred[19,28]{1,0:T(8,128)(4,1)S(1)}, u32[]{:S(2)}) copy-start(pred[19,28]{1,0:T(8,128)(4,1)S(1)} %iota_compare_fusion.16) | copy-start | bytes 1600
  200.4 65.9 %all-gather.19.cloned.1.call-start = ((), (), s32[]{:S(2)}) async-start(), calls=%async_computation.5 | async-start | bytes 1400832 | tf_op jit(solution)/shard_map/all_gather | solution.py:185
  209.5 2.4 copy-start.15
  215.5 85.0 %all-gather.25.cloned.1.call-start = ((), (), s32[]{:S(2)}) async-start(), calls=%async_computation.8 | async-start | bytes 1400832 | tf_op jit(solution)/shard_map/all_gather | solution.py:212
  223.9 11.0 %copy-start.11 = (f32[532,1024]{1,0:T(8,128)S(1)}, f32[532,1024]{1,0:T(8,128)}, u32[]{:S(2)}) copy-start(f32[532,1024]{1,0:T(8,128)} %reshape.489) | copy-start | bytes 6537220
  234.9 4.9 %copy-start.12 = (bf16[1024,2,128]{2,1,0:T(2,128)(2,1)S(1)}, bf16[1024,2,128]{2,1,0:T(2,128)(2,1)}, u32[]{:S(2)}) copy-start(bf16[1024,2,128]{2,1,0:T(2,128)(2,1)} %param.27) | copy-start | bytes 1572868
  234.9 4.9 %copy-start.16 = (f32[1024]{0:T(1024)S(1)}, f32[1024]{0:T(1024)}, u32[]{:S(2)}) copy-start(f32[1024]{0:T(1024)} %param.26) | copy-start | bytes 12292
  240.6 2.3 slice-start.4
  241.8 92.5 %all-gather.21.cloned.1.call-start = ((), (), s32[]{:S(2)}) async-start(), calls=%async_computation.6 | async-start | bytes 1400832 | tf_op jit(solution)/shard_map/all_gather | solution.py:212
  267.7 3.8 %copy-start.13 = (bf16[1024,2,128]{2,1,0:T(2,128)(2,1)S(1)}, bf16[1024,2,128]{2,1,0:T(2,128)(2,1)}, u32[]{:S(2)}) copy-start(bf16[1024,2,128]{2,1,0:T(2,128)(2,1)} %param.27) | copy-start | bytes 1572868
  303.3 33.8 %slice-start.5 = ((pred[19,28]{1,0:T(8,128)(4,1)}), pred[16,28]{1,0:T(8,128)(4,1)S(1)}, s32[]{:S(2)}) async-start(pred[19,28]{1,0:T(8,128)(4,1)} %copy-done.17), calls=%async_computation.14 | async-start | bytes 4096 | tf_op jit(solution)/shard_map/slice | solution.py:150
  334.3 4.0 %copy-start.1 = (bf16[1024,1,384]{2,0,1:T(8,128)(2,1)S(1)}, bf16[1024,1,384]{2,0,1:T(8,128)(2,1)}, u32[]{:S(2)}) copy-start(bf16[1024,1,384]{2,0,1:T(8,128)(2,1)} %param.24) | copy-start | bytes 2359300
  (16 other events, 22.6 us)
Sparse Core Ops, SparseCore 0:
  62.3 28.7 all-gather.16
  93.8 33.4 all-gather.12
  129.4 33.2 all-gather.14
  200.6 32.1 all-gather.22
  234.7 31.5 all-gather.18
  268.9 31.5 all-gather.24
  302.6 31.5 all-gather.20

commit v4 on v1

--- a/solution.py
+++ b/solution.py
@@ -14,6 +14,26 @@
     row_mean = jnp.sum(values, axis=-1, keepdims=True) / model_width
     spread = jnp.sum(values * values, axis=-1, keepdims=True) / model_width - row_mean * row_mean
     return ((values - row_mean) * lax.rsqrt(spread + norm_eps) * gain_cols).astype(jnp.bfloat16)
+
+
+def shifted_terms(block, weight_rows, groups, me):
+    width = block.shape[1]
+    total = jnp.dot(
+        block,
+        lax.dynamic_slice_in_dim(weight_rows, me * width, width, 0),
+        preferred_element_type=jnp.float32,
+    )
+    for shift in range(1, groups):
+        arrived = lax.ppermute(
+            block, "ingest", perm=[(i, (i + shift) % groups) for i in range(groups)]
+        )
+        source = (me + groups - shift) % groups
+        total = total + jnp.dot(
+            arrived,
+            lax.dynamic_slice_in_dim(weight_rows, source * width, width, 0),
+            preferred_element_type=jnp.float32,
+        )
+    return total
 
 
 def shards(
@@ -156,14 +176,8 @@
         "sqk,skd->sqd", probabilities, memory[..., head_dim:], preferred_element_type=jnp.float32
     ).astype(jnp.bfloat16)
 
-    ctx_all = lax.all_gather(context, "ingest", axis=0, tiled=False)
     row_count = utterances * frame_span
-    attn = jnp.einsum(
-        "grc,gcn->rn",
-        ctx_all.reshape(groups, row_count, head_dim),
-        w_out_full.reshape(groups, head_dim, model_width),
-        preferred_element_type=jnp.float32,
-    )
+    attn = shifted_terms(context.reshape(row_count, head_dim), w_out_full, groups, me)
     residual = x_rows.reshape(row_count, model_width) + attn
     normed2 = normalize(residual, ln2_gain)
     mixed = jnp.dot(
@@ -183,12 +197,11 @@
         ].astype(jnp.float32)
     activated = jax.nn.silu(running * bn_scale + bn_shift).astype(jnp.bfloat16)
 
-    act_all = lax.all_gather(activated, "ingest", axis=0, tiled=False)
-    conv_terms = jnp.einsum(
-        "grc,gcn->rn",
-        act_all.reshape(groups, row_count, local_width),
-        w_pw2_cols,
-        preferred_element_type=jnp.float32,
+    conv_terms = shifted_terms(
+        activated.reshape(row_count, local_width),
+        w_pw2_cols.reshape(model_width, local_width),
+        groups,
+        me,
     )
     residual_own = lax.dynamic_slice_in_dim(residual, me * local_width, local_width, 1)
     result = (residual_own + conv_terms).reshape(utterances, frame_span, local_width)

time: 295 us -> 318 us (1.078)
  starting transfers between devices: 28.6 us -> 77.5 us
  waiting for transfers between devices: 185 us -> 139 us
  matrix products: 22.6 us -> 48.6 us
  local copies, waits for them, and re-layouts: 32.4 us -> 26.4 us
    all_gather x2 -> x0, waiting for transfers between devices: 58.5 us -> none  [the longest x1 29.6 us: shards(): act_all = lax.all_gather(activated, 'ingest', axis=0, tiled=False)]
    ppermute x0 -> x14, starting transfers between devices: none -> 49.2 us  [shifted_terms(): lax.ppermute(block, 'ingest', perm=[(i, (i + shift) % groups) for i in ra...]
    dot_general x2 -> x16, matrix products: 6.79 us -> 33.5 us  [the longest x14 28.9 us: shifted_terms(): jnp.dot(arrived, lax.dynamic_slice_in_dim(weight_rows, source * width, wi...]
    ppermute x0 -> x14, waiting for transfers between devices: none -> 16.7 us  [shifted_terms(): lax.ppermute(block, 'ingest', perm=[(i, (i + shift) % groups) for i in ra...]
    all_gather x1, waiting for transfers between devices: 20.3 us -> 14.8 us  [shards(): w_out_full = lax.all_gather(w_out_in, 'ingest', axis=0, tiled=True)]
    reshape x2, local copies, waits for them, and re-layouts: 5.01 us -> 0.1 us  [the longest x1 0.05 us: shards(): context.reshape(row_count, head_dim)]
    unnamed x34 -> x58, local copies, waits for them, and re-layouts: 7.27 us -> 7.98 us
  transfers between devices with their start and end apart: 7 -> 19, of which waited for: 7 -> 10; matrix products, arithmetic and copies ran while one was open for 10% -> 16% of each run, Pallas kernels for 0% -> 0%
where the time goes in v4:
time: 318 us; the launch traced here: 316 us
  waiting for transfers between devices  139 us (44%)
  starting transfers between devices  77.5 us (24%)
  matrix products  48.6 us (15%)
  local copies, waits for them, and re-layouts  26.4 us (8%)
  between operations  14.6 us (5%)
  other arithmetic  10.3 us (3%)
    ppermute x14, starting transfers between devices, shifted_terms(): lax.ppermute(block, 'ingest', perm=[(i, (i + shift) % groups) for i in ra...  49.2 us
    all_gather x1, waiting for transfers between devices, shards(): w_pw2_full = lax.all_gather(w_pw2_in, 'ingest', axis=0, tiled=True)  35.4 us
    all_to_all x1, waiting for transfers between devices, shards(): lax.all_to_all(frame_send, 'owner', split_axis=0, concat_axis=0, tiled=True)  29.3 us
    dot_general x14, matrix products, shifted_terms(): jnp.dot(arrived, lax.dynamic_slice_in_dim(weight_rows, source * width, wi...  28.9 us
    all_to_all x1, waiting for transfers between devices, shards(): lax.all_to_all(cache_send, 'owner', split_axis=0, concat_axis=0, tiled=True)  27 us
    all_to_all x1, starting transfers between devices, shards(): lax.all_to_all(frame_send, 'owner', split_axis=0, concat_axis=0, tiled=True)  19.1 us
    ppermute x14, waiting for transfers between devices, shifted_terms(): lax.ppermute(block, 'ingest', perm=[(i, (i + shift) % groups) for i in ra...  16.7 us
    all_gather x1, waiting for transfers between devices, shards(): x_all = lax.all_gather(arranged, 'ingest', axis=0, tiled=False)  15.2 us
  transfers between devices with their start and end apart: 19, of which 10 were waited for; matrix products, arithmetic and copies ran while one was open for 16% of the time, Pallas kernels for 0%

profile of v4, /device:TPU:1, one launch (start us, length us, event | category | flops | bytes accessed | tf_op | source)
XLA Modules:
  0.0 316.3 jit_solution(10105847324677853319)
XLA Ops:
  11.4 19.1 %all-to-all-start = ((bf16[64,32,128]{2,1,0:T(8,128)(2,1)}), bf16[64,32,128]{2,1,0:T(8,128)(2,1)S(1)}, u32[]{:S(2)}, u32[]{:S(2)}) async-start(bf16[64,32,128]{2,1,0:T(8,128)(2,1)} %copy.52), calls=%async_computation | async-start | bytes 1048576 | tf_op jit(solution)/shard_map/all_to_all | solution.py:89
  30.5 29.3 %all-to-all-done = bf16[64,32,128]{2,1,0:T(8,128)(2,1)S(1)} async-done(((bf16[64,32,128]{2,1,0:T(8,128)(2,1)}), bf16[64,32,128]{2,1,0:T(8,128)(2,1)S(1)}, u32[]{:S(2)}, u32[]{:S(2)}) %all-to-all-start) | async-done | bytes 524320 | tf_op jit(solution)/shard_map/all_to_all | solution.py:89
  64.0 3.0 copy.60
  67.0 8.9 %all-to-all-start.1 = ((bf16[64,80,256]{2,1,0:T(8,128)(2,1)}), bf16[64,80,256]{2,1,0:T(8,128)(2,1)}, u32[]{:S(2)}, u32[]{:S(2)}) async-start(bf16[64,80,256]{2,1,0:T(8,128)(2,1)} %copy.60), calls=%async_computation.1 | async-start | bytes 5242880 | tf_op jit(solution)/shard_map/all_to_all | solution.py:114
  75.9 15.2 %all-gather.9.cloned.1.call-done = bf16[264,28,128]{2,1,0:T(8,128)(2,1)} async-done(((bf16[33,28,128]{2,1,0:T(8,128)(2,1)}), bf16[264,28,128]{2,1,0:T(8,128)(2,1)}) %all-gather.9.cloned.1.call-update) | async-done | bytes 1892368 | tf_op jit(solution)/shard_map/all_gather | solution.py:125
  100.2 4.1 %convert_element_type.199 = bf16[33,28,1024]{2,1,0:T(8,128)(2,1)} reshape(bf16[33,28,8,128]{3,2,1,0:T(8,128)(2,1)} %copy.57) | data formatting | bytes 3784704 | tf_op jit(solution)/shard_map/convert_element_type | solution.py:16
  104.3 2.9 convolution_convert_fusion.1
  109.7 2.8 copy.73
  112.4 14.8 %all-gather.5.cloned.1.call-done = bf16[1024,1024]{1,0:T(8,128)(2,1)} async-done(((bf16[128,1024]{1,0:T(8,128)(2,1)}), bf16[1024,1024]{1,0:T(8,128)(2,1)}) %all-gather.5.cloned.1.call-update) | async-done | bytes 2097168 | tf_op jit(solution)/shard_map/all_gather | solution.py:127
  127.2 35.4 %all-gather.7.cloned.1.call-done = bf16[1024,1024]{1,0:T(8,128)(2,1)} async-done(((bf16[128,1024]{1,0:T(8,128)(2,1)}), bf16[1024,1024]{1,0:T(8,128)(2,1)}) %all-gather.7.cloned.1.call-update) | async-done | bytes 2097168 | tf_op jit(solution)/shard_map/all_gather | solution.py:128
  162.9 27.0 %all-to-all-done.1 = bf16[64,80,256]{2,1,0:T(8,128)(2,1)} async-done(((bf16[64,80,256]{2,1,0:T(8,128)(2,1)}), bf16[64,80,256]{2,1,0:T(8,128)(2,1)}, u32[]{:S(2)}, u32[]{:S(2)}) %all-to-all-start.1) | async-done | bytes 2621472 | tf_op jit(solution)/shard_map/all_to_all | solution.py:114
  198.7 3.1 convolution_convert_fusion.4
  201.9 7.6 %collective-permute-start.6 = (bf16[924,128]{1,0:T(8,128)(2,1)S(1)}, bf16[924,128]{1,0:T(8,128)(2,1)S(1)}, u32[]{:S(2)}, u32[]{:S(2)}) collective-permute-start(bf16[924,128]{1,0:T(8,128)(2,1)S(1)} %reshape.335), channel_id=1, source_target_pairs={{0,448},{64,0},{128,64},{192,128},{256,192},{320,256},{384,320},{4... | collective-permute-start | bytes 709640 | tf_op jit(solution)/shard_map/ppermute | solution.py:27
  209.5 4.6 %collective-permute-start.5 = (bf16[924,128]{1,0:T(8,128)(2,1)S(1)}, bf16[924,128]{1,0:T(8,128)(2,1)S(1)}, u32[]{:S(2)}, u32[]{:S(2)}) collective-permute-start(bf16[924,128]{1,0:T(8,128)(2,1)S(1)} %reshape.335), channel_id=1, source_target_pairs={{0,384},{64,448},{128,0},{192,64},{256,128},{320,192},{384,256},{4... | collective-permute-start | bytes 709640 | tf_op jit(solution)/shard_map/ppermute | solution.py:27
  220.5 3.5 %fusion.78 = f32[924,1024]{1,0:T(8,128)} fusion(bf16[924,128]{1,0:T(8,128)(2,1)S(1)} %reshape.335, bf16[1024,1024]{1,0:T(8,128)(2,1)} %all-gather.5.cloned.1.call-done, s32[]{:T(128)S(6)} %select_n.120), kind=kOutput, calls=%fused_computation.104 | convolution fusion | flops 242221056 | bytes 4283396 | tf_op jit(solution)/shard_map/dot_general | solution.py:21
  227.7 3.1 collective-permute-start.1
  232.4 3.3 %collective-permute-done.1 = bf16[924,128]{1,0:T(8,128)(2,1)S(1)} collective-permute-done((bf16[924,128]{1,0:T(8,128)(2,1)S(1)}, bf16[924,128]{1,0:T(8,128)(2,1)S(1)}, u32[]{:S(2)}, u32[]{:S(2)}) %collective-permute-start.1) | collective-permute-done | bytes 236576 | tf_op jit(solution)/shard_map/ppermute | solution.py:27
  235.8 6.4 %collective-permute-start.2 = (bf16[924,128]{1,0:T(8,128)(2,1)S(1)}, bf16[924,128]{1,0:T(8,128)(2,1)S(1)}, u32[]{:S(2)}, u32[]{:S(2)}) collective-permute-start(bf16[924,128]{1,0:T(8,128)(2,1)S(1)} %reshape.335), channel_id=1, source_target_pairs={{0,192},{64,256},{128,320},{192,384},{256,448},{320,0},{384,64},{4... | collective-permute-start | bytes 709640 | tf_op jit(solution)/shard_map/ppermute | solution.py:27
  242.9 4.4 %collective-permute-done.2 = bf16[924,128]{1,0:T(8,128)(2,1)S(1)} collective-permute-done((bf16[924,128]{1,0:T(8,128)(2,1)S(1)}, bf16[924,128]{1,0:T(8,128)(2,1)S(1)}, u32[]{:S(2)}, u32[]{:S(2)}) %collective-permute-start.2) | collective-permute-done | bytes 236576 | tf_op jit(solution)/shard_map/ppermute | solution.py:27
  258.1 8.1 %fusion.128 = (f32[924]{0:T(1024)S(1)}, f32[924]{0:T(1024)S(1)}, f32[924,1024]{1,0:T(8,128)S(1)}) fusion(f32[924,1024]{1,0:T(8,128)S(1)} %bitcast.95, bf16[924,128]{1,0:T(8,128)(2,1)S(1)} %collective-permute-done.6, bf16[1024,1024]{1,0:T(8,128)(2,1)} %all-gather.5.cloned.1.call-done, s32[]{:T(128)S(6)} %select_n.134, f32[924,1024]{1,0:T(8,128)} %fusion.66, ...), kind=kOutput, calls=%fused_computation.183 | convolution fusion | flops 252627136 | bytes 34633956 | tf_op jit(solution)/shard_map/dot_general | solution.py:31
  273.9 4.6 %collective-permute-start.11 = (bf16[924,128]{1,0:T(8,128)(2,1)S(1)}, bf16[924,128]{1,0:T(8,128)(2,1)S(1)}, u32[]{:S(2)}, u32[]{:S(2)}) collective-permute-start(bf16[924,128]{1,0:T(8,128)(2,1)S(1)} %reshape.339), channel_id=1, source_target_pairs={{0,320},{64,384},{128,448},{192,0},{256,64},{320,128},{384,192},{4... | collective-permute-start | bytes 709640 | tf_op jit(solution)/shard_map/ppermute | solution.py:27
  284.8 4.5 %collective-permute-done.7 = bf16[924,128]{1,0:T(8,128)(2,1)S(1)} collective-permute-done((bf16[924,128]{1,0:T(8,128)(2,1)S(1)}, bf16[924,128]{1,0:T(8,128)(2,1)S(1)}, u32[]{:S(2)}, u32[]{:S(2)}) %collective-permute-start.7) | collective-permute-done | bytes 236576 | tf_op jit(solution)/shard_map/ppermute | solution.py:27
  289.4 5.8 %collective-permute-start.9 = (bf16[924,128]{1,0:T(8,128)(2,1)S(1)}, bf16[924,128]{1,0:T(8,128)(2,1)S(1)}, u32[]{:S(2)}, u32[]{:S(2)}) collective-permute-start(bf16[924,128]{1,0:T(8,128)(2,1)S(1)} %reshape.339), channel_id=1, source_target_pairs={{0,192},{64,256},{128,320},{192,384},{256,448},{320,0},{384,64},{4... | collective-permute-start | bytes 709640 | tf_op jit(solution)/shard_map/ppermute | solution.py:27
  304.5 2.9 collective-permute-done.8
  (160 shorter events, 77.2 us)
Async XLA Ops:
  7.2 97.1 %copy-start = (bf16[1024,1,384]{2,0,1:T(8,128)(2,1)S(1)}, bf16[1024,1,384]{2,0,1:T(8,128)(2,1)}, u32[]{:S(2)}) copy-start(bf16[1024,1,384]{2,0,1:T(8,128)(2,1)} %param.24) | copy-start | bytes 2359300
  9.0 53.3 %slice-start.2 = ((bf16[33,8,128]{2,1,0:T(8,128)(2,1)}), bf16[32,8,128]{2,1,0:T(8,128)(2,1)S(1)}, s32[]{:S(2)}) async-start(bf16[33,8,128]{2,1,0:T(8,128)(2,1)} %param.21), calls=%async_computation.7 | async-start | bytes 131072 | tf_op jit(solution)/shard_map/slice | solution.py:102
  11.4 48.5 %all-to-all-start = ((bf16[64,32,128]{2,1,0:T(8,128)(2,1)}), bf16[64,32,128]{2,1,0:T(8,128)(2,1)S(1)}, u32[]{:S(2)}, u32[]{:S(2)}) async-start(bf16[64,32,128]{2,1,0:T(8,128)(2,1)} %copy.52), calls=%async_computation | async-start | bytes 1048576 | tf_op jit(solution)/shard_map/all_to_all | solution.py:89
  30.5 31.9 %slice-start.1 = ((bf16[33,1,70,256]{3,2,1,0:T(8,128)(2,1)}), bf16[32,1,70,256]{3,2,1,0:T(8,128)(2,1)S(1)}, s32[]{:S(2)}) async-start(bf16[33,1,70,256]{3,2,1,0:T(8,128)(2,1)} %param.20), calls=%async_computation.6 | async-start | bytes 2359296 | tf_op jit(solution)/shard_map/slice | solution.py:101
  30.5 60.6 %all-gather.9.cloned.1.call-start = ((), (), s32[]{:S(2)}) async-start(), calls=%async_computation.4 | async-start | bytes 2433024 | tf_op jit(solution)/shard_map/all_gather | solution.py:125
  67.0 122.9 %all-to-all-start.1 = ((bf16[64,80,256]{2,1,0:T(8,128)(2,1)}), bf16[64,80,256]{2,1,0:T(8,128)(2,1)}, u32[]{:S(2)}, u32[]{:S(2)}) async-start(bf16[64,80,256]{2,1,0:T(8,128)(2,1)} %copy.60), calls=%async_computation.1 | async-start | bytes 5242880 | tf_op jit(solution)/shard_map/all_to_all | solution.py:114
  75.9 51.3 %all-gather.5.cloned.1.call-start = ((), (), s32[]{:S(2)}) async-start(), calls=%async_computation.2 | async-start | bytes 2359296 | tf_op jit(solution)/shard_map/all_gather | solution.py:127
  93.6 69.0 %all-gather.7.cloned.1.call-start = ((), (), s32[]{:S(2)}) async-start(), calls=%async_computation.3 | async-start | bytes 2359296 | tf_op jit(solution)/shard_map/all_gather | solution.py:128
  109.6 53.0 %copy-start.6 = (bf16[33,28,256]{2,1,0:T(8,128)(2,1)S(1)}, bf16[33,28,256]{2,1,0:T(8,128)(2,1)}, u32[]{:S(2)}) copy-start(bf16[33,28,256]{2,1,0:T(8,128)(2,1)} %slice.141) | copy-start | bytes 1419268
  201.8 22.2 %slice-start = ((bf16[32,74,256]{2,0,1:T(8,128)(2,1)}), bf16[32,4,256]{2,0,1:T(8,128)(2,1)S(1)}, s32[]{:S(2)}) async-start(bf16[32,74,256]{2,0,1:T(8,128)(2,1)} %copy-done.5), calls=%async_computation.5 | async-start | bytes 131072 | tf_op jit(solution)/shard_map/slice | solution.py:154
  201.9 55.4 %collective-permute-start.6 = (bf16[924,128]{1,0:T(8,128)(2,1)S(1)}, bf16[924,128]{1,0:T(8,128)(2,1)S(1)}, u32[]{:S(2)}, u32[]{:S(2)}) collective-permute-start(bf16[924,128]{1,0:T(8,128)(2,1)S(1)} %reshape.335), channel_id=1, source_target_pairs={{0,448},{64,0},{128,64},{192,128},{256,192},{320,256},{384,320},{4... | collective-permute-start | bytes 709640 | tf_op jit(solution)/shard_map/ppermute | solution.py:27
  209.5 45.3 %collective-permute-start.5 = (bf16[924,128]{1,0:T(8,128)(2,1)S(1)}, bf16[924,128]{1,0:T(8,128)(2,1)S(1)}, u32[]{:S(2)}, u32[]{:S(2)}) collective-permute-start(bf16[924,128]{1,0:T(8,128)(2,1)S(1)} %reshape.335), channel_id=1, source_target_pairs={{0,384},{64,448},{128,0},{192,64},{256,128},{320,192},{384,256},{4... | collective-permute-start | bytes 709640 | tf_op jit(solution)/shard_map/ppermute | solution.py:27
  214.2 38.1 %collective-permute-start.4 = (bf16[924,128]{1,0:T(8,128)(2,1)S(1)}, bf16[924,128]{1,0:T(8,128)(2,1)S(1)}, u32[]{:S(2)}, u32[]{:S(2)}) collective-permute-start(bf16[924,128]{1,0:T(8,128)(2,1)S(1)} %reshape.335), channel_id=1, source_target_pairs={{0,320},{64,384},{128,448},{192,0},{256,64},{320,128},{384,192},{4... | collective-permute-start | bytes 709640 | tf_op jit(solution)/shard_map/ppermute | solution.py:27
  216.7 33.0 %collective-permute-start.3 = (bf16[924,128]{1,0:T(8,128)(2,1)S(1)}, bf16[924,128]{1,0:T(8,128)(2,1)S(1)}, u32[]{:S(2)}, u32[]{:S(2)}) collective-permute-start(bf16[924,128]{1,0:T(8,128)(2,1)S(1)} %reshape.335), channel_id=1, source_target_pairs={{0,256},{64,320},{128,384},{192,448},{256,0},{320,64},{384,128},{4... | collective-permute-start | bytes 709640 | tf_op jit(solution)/shard_map/ppermute | solution.py:27
  218.9 8.8 %collective-permute-start = (bf16[924,128]{1,0:T(8,128)(2,1)S(1)}, bf16[924,128]{1,0:T(8,128)(2,1)}, u32[]{:S(2)}, u32[]{:S(2)}) collective-permute-start(bf16[924,128]{1,0:T(8,128)(2,1)S(1)} %reshape.335), channel_id=1, source_target_pairs={{0,64},{64,128},{128,192},{192,256},{256,320},{320,384},{384,448},... | collective-permute-start | bytes 709640 | tf_op jit(solution)/shard_map/ppermute | solution.py:27
  227.7 8.1 %collective-permute-start.1 = (bf16[924,128]{1,0:T(8,128)(2,1)S(1)}, bf16[924,128]{1,0:T(8,128)(2,1)S(1)}, u32[]{:S(2)}, u32[]{:S(2)}) collective-permute-start(bf16[924,128]{1,0:T(8,128)(2,1)S(1)} %reshape.335), channel_id=1, source_target_pairs={{0,128},{64,192},{128,256},{192,320},{256,384},{320,448},{384,0},{... | collective-permute-start | bytes 709640 | tf_op jit(solution)/shard_map/ppermute | solution.py:27
  235.8 11.5 %collective-permute-start.2 = (bf16[924,128]{1,0:T(8,128)(2,1)S(1)}, bf16[924,128]{1,0:T(8,128)(2,1)S(1)}, u32[]{:S(2)}, u32[]{:S(2)}) collective-permute-start(bf16[924,128]{1,0:T(8,128)(2,1)S(1)} %reshape.335), channel_id=1, source_target_pairs={{0,192},{64,256},{128,320},{192,384},{256,448},{320,0},{384,64},{4... | collective-permute-start | bytes 709640 | tf_op jit(solution)/shard_map/ppermute | solution.py:27
  269.6 26.8 %collective-permute-start.13 = (bf16[924,128]{1,0:T(8,128)(2,1)S(1)}, bf16[924,128]{1,0:T(8,128)(2,1)S(1)}, u32[]{:S(2)}, u32[]{:S(2)}) collective-permute-start(bf16[924,128]{1,0:T(8,128)(2,1)S(1)} %reshape.339), channel_id=1, source_target_pairs={{0,448},{64,0},{128,64},{192,128},{256,192},{320,256},{384,320},{4... | collective-permute-start | bytes 709640 | tf_op jit(solution)/shard_map/ppermute | solution.py:27
  272.0 27.6 %collective-permute-start.12 = (bf16[924,128]{1,0:T(8,128)(2,1)S(1)}, bf16[924,128]{1,0:T(8,128)(2,1)S(1)}, u32[]{:S(2)}, u32[]{:S(2)}) collective-permute-start(bf16[924,128]{1,0:T(8,128)(2,1)S(1)} %reshape.339), channel_id=1, source_target_pairs={{0,384},{64,448},{128,0},{192,64},{256,128},{320,192},{384,256},{4... | collective-permute-start | bytes 709640 | tf_op jit(solution)/shard_map/ppermute | solution.py:27
  273.9 26.9 %collective-permute-start.11 = (bf16[924,128]{1,0:T(8,128)(2,1)S(1)}, bf16[924,128]{1,0:T(8,128)(2,1)S(1)}, u32[]{:S(2)}, u32[]{:S(2)}) collective-permute-start(bf16[924,128]{1,0:T(8,128)(2,1)S(1)} %reshape.339), channel_id=1, source_target_pairs={{0,320},{64,384},{128,448},{192,0},{256,64},{320,128},{384,192},{4... | collective-permute-start | bytes 709640 | tf_op jit(solution)/shard_map/ppermute | solution.py:27
  278.5 23.5 %collective-permute-start.10 = (bf16[924,128]{1,0:T(8,128)(2,1)S(1)}, bf16[924,128]{1,0:T(8,128)(2,1)S(1)}, u32[]{:S(2)}, u32[]{:S(2)}) collective-permute-start(bf16[924,128]{1,0:T(8,128)(2,1)S(1)} %reshape.339), channel_id=1, source_target_pairs={{0,256},{64,320},{128,384},{192,448},{256,0},{320,64},{384,128},{4... | collective-permute-start | bytes 709640 | tf_op jit(solution)/shard_map/ppermute | solution.py:27
  281.2 8.2 %collective-permute-start.7 = (bf16[924,128]{1,0:T(8,128)(2,1)S(1)}, bf16[924,128]{1,0:T(8,128)(2,1)S(1)}, u32[]{:S(2)}, u32[]{:S(2)}) collective-permute-start(bf16[924,128]{1,0:T(8,128)(2,1)S(1)} %reshape.339), channel_id=1, source_target_pairs={{0,64},{64,128},{128,192},{192,256},{256,320},{320,384},{384,448},... | collective-permute-start | bytes 709640 | tf_op jit(solution)/shard_map/ppermute | solution.py:27
  289.4 13.8 %collective-permute-start.9 = (bf16[924,128]{1,0:T(8,128)(2,1)S(1)}, bf16[924,128]{1,0:T(8,128)(2,1)S(1)}, u32[]{:S(2)}, u32[]{:S(2)}) collective-permute-start(bf16[924,128]{1,0:T(8,128)(2,1)S(1)} %reshape.339), channel_id=1, source_target_pairs={{0,192},{64,256},{128,320},{192,384},{256,448},{320,0},{384,64},{4... | collective-permute-start | bytes 709640 | tf_op jit(solution)/shard_map/ppermute | solution.py:27
  296.4 10.9 %collective-permute-start.8 = (bf16[924,128]{1,0:T(8,128)(2,1)S(1)}, bf16[924,128]{1,0:T(8,128)(2,1)S(1)}, u32[]{:S(2)}, u32[]{:S(2)}) collective-permute-start(bf16[924,128]{1,0:T(8,128)(2,1)S(1)} %reshape.339), channel_id=1, source_target_pairs={{0,128},{64,192},{128,256},{192,320},{256,384},{320,448},{384,0},{... | collective-permute-start | bytes 709640 | tf_op jit(solution)/shard_map/ppermute | solution.py:27
  (25 other events, 68.4 us)
Sparse Core Ops, SparseCore 0:
  62.3 28.7 all-gather.8
  93.7 33.4 all-gather.4
  129.4 33.2 all-gather.6

commit v5 on v1

--- a/solution.py
+++ b/solution.py
@@ -66,7 +66,6 @@
         frame_rows_tagged,
         preferred_element_type=jnp.float32,
     ).astype(jnp.bfloat16)
-    frame_got = lax.all_to_all(frame_send, "owner", split_axis=0, concat_axis=0, tiled=True)
 
     kv_lanes = 2 * head_dim
     conv_fold = conv_len * local_width // kv_lanes
@@ -91,6 +90,8 @@
         cache_rows,
         preferred_element_type=jnp.float32,
     ).astype(jnp.bfloat16)
+    frame_send = frame_send + 0 * cache_send[:, : frame_send.shape[1], : frame_send.shape[2]]
+    frame_got = lax.all_to_all(frame_send, "owner", split_axis=0, concat_axis=0, tiled=True)
     cache_got = lax.all_to_all(cache_send, "owner", split_axis=0, concat_axis=0, tiled=True)
 
     got_slot = frame_got[:, frame_span, 0].astype(jnp.int32)
@@ -106,16 +107,15 @@
     w_out_in, w_pw2_in, x_all = lax.optimization_barrier((w_out, w_pw2, x_all))
     w_out_full = lax.all_gather(w_out_in, "ingest", axis=0, tiled=True)
     w_pw2_full = lax.all_gather(w_pw2_in, "ingest", axis=0, tiled=True)
-    x_rows = x_all.transpose(1, 2, 0, 3).reshape(utterances, frame_span, model_width)
-    x_rows = x_rows.astype(jnp.float32)
-    normed = normalize(x_rows, ln1_gain)
+    x_plain = x_all.transpose(1, 2, 0, 3).reshape(utterances, frame_span, model_width)
+    normed = normalize(x_plain.astype(jnp.float32), ln1_gain)
     projected = jnp.dot(
         normed, w_qkv.reshape(model_width, 3 * head_dim), preferred_element_type=jnp.float32
     )
     queries = projected[..., :head_dim].astype(jnp.bfloat16)
     fresh = projected[..., head_dim:].astype(jnp.bfloat16)
-    w_out_full, w_pw2_full, queries, fresh = lax.optimization_barrier(
-        (w_out_full, w_pw2_full, queries, fresh)
+    w_out_full, w_pw2_full, x_plain, queries, fresh = lax.optimization_barrier(
+        (w_out_full, w_pw2_full, x_plain, queries, fresh)
     )
     w_pw2_cols = lax.dynamic_slice_in_dim(w_pw2_full, me * local_width, local_width, 1).reshape(
         groups, local_width, local_width
@@ -164,7 +164,7 @@
         w_out_full.reshape(groups, head_dim, model_width),
         preferred_element_type=jnp.float32,
     )
-    residual = x_rows.reshape(row_count, model_width) + attn
+    residual = x_plain.reshape(row_count, model_width).astype(jnp.float32) + attn
     normed2 = normalize(residual, ln2_gain)
     mixed = jnp.dot(
         normed2, w_pw1.reshape(model_width, 2 * local_width), preferred_element_type=jnp.float32

time: 295 us -> 298 us (1.010)
  local copies, waits for them, and re-layouts: 32.4 us -> 40.5 us
  waiting for transfers between devices: 185 us -> 179 us
    all_gather x1, waiting for transfers between devices: 20.3 us -> 13.8 us  [shards(): w_out_full = lax.all_gather(w_out_in, 'ingest', axis=0, tiled=True)]
    reshape x0 -> x1, local copies, waits for them, and re-layouts: none -> 4.25 us  [shards(): x_all.transpose(1, 2, 0, 3).reshape(utterances, frame_span, model_width)]
    unnamed x34 -> x30, local copies, waits for them, and re-layouts: 7.27 us -> 4.12 us
  transfers between devices with their start and end apart: 7 -> 7, of which waited for: 7 -> 7; matrix products, arithmetic and copies ran while one was open for 10% -> 11% of each run, Pallas kernels for 0% -> 0%
where the time goes in v5:
time: 298 us; the launch traced here: 297 us
  waiting for transfers between devices  179 us (60%)
  local copies, waits for them, and re-layouts  40.5 us (14%)
  starting transfers between devices  28.9 us (10%)
  matrix products  23.6 us (8%)
  between operations  14.1 us (5%)
  other arithmetic  10.8 us (4%)
    all_gather x1, waiting for transfers between devices, shards(): w_pw2_full = lax.all_gather(w_pw2_in, 'ingest', axis=0, tiled=True)  35.4 us
    all_gather x1, waiting for transfers between devices, shards(): act_all = lax.all_gather(activated, 'ingest', axis=0, tiled=False)  29.6 us
    all_to_all x1, waiting for transfers between devices, shards(): lax.all_to_all(frame_send, 'owner', split_axis=0, concat_axis=0, tiled=True)  29.2 us
    all_gather x1, waiting for transfers between devices, shards(): ctx_all = lax.all_gather(context, 'ingest', axis=0, tiled=False)  28.5 us
    all_to_all x1, waiting for transfers between devices, shards(): lax.all_to_all(cache_send, 'owner', split_axis=0, concat_axis=0, tiled=True)  25.2 us
    all_to_all x1, starting transfers between devices, shards(): lax.all_to_all(frame_send, 'owner', split_axis=0, concat_axis=0, tiled=True)  19.4 us
    all_gather x1, waiting for transfers between devices, shards(): x_all = lax.all_gather(arranged, 'ingest', axis=0, tiled=False)  17 us
    all_gather x1, waiting for transfers between devices, shards(): w_out_full = lax.all_gather(w_out_in, 'ingest', axis=0, tiled=True)  13.8 us
  transfers between devices with their start and end apart: 7, of which 7 were waited for; matrix products, arithmetic and copies ran while one was open for 11% of the time, Pallas kernels for 0%

profile of v5, /device:TPU:1, one launch (start us, length us, event | category | flops | bytes accessed | tf_op | source)
XLA Modules:
  0.0 297.2 jit_solution(16390521641850589209)
XLA Ops:
  13.4 19.4 %all-to-all-start = ((bf16[64,32,128]{2,1,0:T(8,128)(2,1)}), bf16[64,32,128]{2,1,0:T(8,128)(2,1)}, u32[]{:S(2)}, u32[]{:S(2)}) async-start(bf16[64,32,128]{2,1,0:T(8,128)(2,1)} %copy.53), calls=%async_computation | async-start | bytes 1048576 | tf_op jit(solution)/shard_map/all_to_all | solution.py:94
  32.8 29.2 %all-to-all-done = bf16[64,32,128]{2,1,0:T(8,128)(2,1)} async-done(((bf16[64,32,128]{2,1,0:T(8,128)(2,1)}), bf16[64,32,128]{2,1,0:T(8,128)(2,1)}, u32[]{:S(2)}, u32[]{:S(2)}) %all-to-all-start) | async-done | bytes 524320 | tf_op jit(solution)/shard_map/all_to_all | solution.py:94
  62.0 2.1 fusion.66
  66.3 3.0 %copy.59 = bf16[64,80,256]{2,1,0:T(8,128)(2,1)} copy(bf16[64,80,256]{2,0,1:T(8,128)(2,1)S(1)} %convolution_convert_fusion) | data formatting | bytes 5242880 | tf_op jit(solution)/shard_map/convert_element_type | solution.py:92
  69.2 8.9 %all-to-all-start.1 = ((bf16[64,80,256]{2,1,0:T(8,128)(2,1)}), bf16[64,80,256]{2,1,0:T(8,128)(2,1)}, u32[]{:S(2)}, u32[]{:S(2)}) async-start(bf16[64,80,256]{2,1,0:T(8,128)(2,1)} %copy.59), calls=%async_computation.1 | async-start | bytes 5242880 | tf_op jit(solution)/shard_map/all_to_all | solution.py:95
  78.2 17.0 %all-gather.13.cloned.1.call-done = bf16[264,28,128]{2,1,0:T(8,128)(2,1)} async-done(((bf16[33,28,128]{2,1,0:T(8,128)(2,1)}), bf16[264,28,128]{2,1,0:T(8,128)(2,1)}) %all-gather.13.cloned.1.call-update) | async-done | bytes 1892368 | tf_op jit(solution)/shard_map/all_gather | solution.py:106
  95.2 2.4 copy.68
  103.0 4.2 %convert_element_type.194 = bf16[33,28,1024]{2,1,0:T(8,128)(2,1)} reshape(bf16[33,28,8,128]{3,2,1,0:T(8,128)(2,1)} %copy.58) | data formatting | bytes 3784704 | tf_op jit(solution)/shard_map/convert_element_type | solution.py:16
  107.1 2.9 convolution_convert_fusion.1
  113.2 4.3 %reshape.341 = bf16[33,28,1024]{2,1,0:T(8,128)(2,1)} reshape(bf16[33,28,8,128]{3,2,1,0:T(8,128)(2,1)} %copy.57) | data formatting | bytes 3784704 | tf_op jit(solution)/shard_map/reshape | solution.py:110
  117.5 13.8 %all-gather.9.cloned.1.call-done = bf16[1024,1024]{1,0:T(8,128)(2,1)} async-done(((bf16[128,1024]{1,0:T(8,128)(2,1)}), bf16[1024,1024]{1,0:T(8,128)(2,1)}) %all-gather.9.cloned.1.call-update) | async-done | bytes 2097168 | tf_op jit(solution)/shard_map/all_gather | solution.py:108
  131.3 35.4 %all-gather.11.cloned.1.call-done = bf16[1024,1024]{1,0:T(8,128)(2,1)} async-done(((bf16[128,1024]{1,0:T(8,128)(2,1)}), bf16[1024,1024]{1,0:T(8,128)(2,1)}) %all-gather.11.cloned.1.call-update) | async-done | bytes 2097168 | tf_op jit(solution)/shard_map/all_gather | solution.py:109
  166.9 25.2 %all-to-all-done.1 = bf16[64,80,256]{2,1,0:T(8,128)(2,1)} async-done(((bf16[64,80,256]{2,1,0:T(8,128)(2,1)}), bf16[64,80,256]{2,1,0:T(8,128)(2,1)}, u32[]{:S(2)}, u32[]{:S(2)}) %all-to-all-start.1) | async-done | bytes 2621472 | tf_op jit(solution)/shard_map/all_to_all | solution.py:95
  192.2 2.1 fusion.65
  194.3 2.6 fusion.16
  201.1 3.8 %convolution_convert_fusion.4 = bf16[33,28,128]{2,1,0:T(8,128)(2,1)} fusion(bf16[33,98,128]{2,0,1:T(8,128)(2,1)} %get-tuple-element.36, f32[33,28]{1,0:T(8,128)S(1)} %fusion.88, f32[33,28,98]{2,1,0:T(8,128)S(1)} %fusion.30), kind=kOutput, calls=%fused_computation.40 | convolution fusion | flops 23572260 | bytes 1430352 | tf_op jit(solution)/shard_map/sqk,skd->sqd/dot_general | solution.py:155
  205.9 4.1 %reshape.353 = f32[924,1024]{1,0:T(8,128)} reshape(bf16[33,28,1024]{2,1,0:T(8,128)(2,1)} %reshape.341) | data formatting | bytes 5677056 | tf_op jit(solution)/shard_map/convert_element_type | solution.py:167
  210.1 28.5 %all-gather.15.cloned.1.call-done = bf16[264,28,128]{2,1,0:T(8,128)(2,1)} async-done(((bf16[33,28,128]{2,1,0:T(8,128)(2,1)}), bf16[264,28,128]{2,1,0:T(8,128)(2,1)}) %all-gather.15.cloned.1.call-update) | async-done | bytes 1892368 | tf_op jit(solution)/shard_map/all_gather | solution.py:159
  238.6 3.7 %reshape.343 = bf16[8,924,128]{2,1,0:T(8,128)(2,1)} reshape(bf16[264,28,128]{2,1,0:T(8,128)(2,1)} %all-gather.15.cloned.1.call-done) | data formatting | bytes 3784704 | tf_op jit(solution)/shard_map/reshape | solution.py:163
  242.3 5.7 %fusion.86 = (f32[924]{0:T(1024)S(1)}, f32[924]{0:T(1024)S(1)}, f32[924,1024]{1,0:T(8,128)S(1)}) fusion(f32[924,1024]{1,0:T(8,128)} %reshape.353, bf16[8,924,128]{2,1,0:T(8,128)(2,1)} %reshape.343, bf16[8,128,1024]{2,1,0:T(8,128)(2,1)} %bitcast.90), kind=kOutput, calls=%fused_computation.145 | convolution fusion | flops 1941551360 | bytes 11566304 | tf_op jit(solution)/shard_map/grc,gcn->rn/dot_general | solution.py:161
  253.1 2.0 fusion.19
  256.0 29.6 %all-gather.17.cloned.1.call-done = bf16[264,28,128]{2,1,0:T(8,128)(2,1)} async-done(((bf16[33,28,128]{2,1,0:T(8,128)(2,1)}), bf16[264,28,128]{2,1,0:T(8,128)(2,1)}) %all-gather.17.cloned.1.call-update) | async-done | bytes 1892368 | tf_op jit(solution)/shard_map/all_gather | solution.py:186
  285.6 2.5 reshape.348
  288.1 1.7 fusion.32
  (97 shorter events, 29.3 us)
Async XLA Ops:
  7.2 100.0 %copy-start = (bf16[1024,1,384]{2,0,1:T(8,128)(2,1)S(1)}, bf16[1024,1,384]{2,0,1:T(8,128)(2,1)}, u32[]{:S(2)}) copy-start(bf16[1024,1,384]{2,0,1:T(8,128)(2,1)} %param.24) | copy-start | bytes 2359300
  7.2 3.0 %slice-start.1 = ((bf16[33,1,70,256]{3,2,1,0:T(8,128)(2,1)}), bf16[32,1,70,256]{3,2,1,0:T(8,128)(2,1)S(1)}, s32[]{:S(2)}) async-start(bf16[33,1,70,256]{3,2,1,0:T(8,128)(2,1)} %param.20), calls=%async_computation.8 | async-start | bytes 2359296 | tf_op jit(solution)/shard_map/slice | solution.py:80
  10.1 0.7 copy-start.10
  10.4 1.4 copy-start.13
  13.4 48.6 %all-to-all-start = ((bf16[64,32,128]{2,1,0:T(8,128)(2,1)}), bf16[64,32,128]{2,1,0:T(8,128)(2,1)}, u32[]{:S(2)}, u32[]{:S(2)}) async-start(bf16[64,32,128]{2,1,0:T(8,128)(2,1)} %copy.53), calls=%async_computation | async-start | bytes 1048576 | tf_op jit(solution)/shard_map/all_to_all | solution.py:94
  32.8 62.4 %all-gather.13.cloned.1.call-start = ((), (), s32[]{:S(2)}) async-start(), calls=%async_computation.4 | async-start | bytes 2433024 | tf_op jit(solution)/shard_map/all_gather | solution.py:106
  69.2 122.9 %all-to-all-start.1 = ((bf16[64,80,256]{2,1,0:T(8,128)(2,1)}), bf16[64,80,256]{2,1,0:T(8,128)(2,1)}, u32[]{:S(2)}, u32[]{:S(2)}) async-start(bf16[64,80,256]{2,1,0:T(8,128)(2,1)} %copy.59), calls=%async_computation.1 | async-start | bytes 5242880 | tf_op jit(solution)/shard_map/all_to_all | solution.py:95
  78.1 53.1 %all-gather.9.cloned.1.call-start = ((), (), s32[]{:S(2)}) async-start(), calls=%async_computation.2 | async-start | bytes 2359296 | tf_op jit(solution)/shard_map/all_gather | solution.py:108
  95.2 4.4 %copy-start.6 = (s32[33]{0:T(128)S(1)}, s32[33]{0:T(128)}, u32[]{:S(2)}) copy-start(s32[33]{0:T(128)} %param.19) | copy-start | bytes 400
  97.6 2.9 copy-start.8
  97.7 69.0 %all-gather.11.cloned.1.call-start = ((), (), s32[]{:S(2)}) async-start(), calls=%async_computation.3 | async-start | bytes 2359296 | tf_op jit(solution)/shard_map/all_gather | solution.py:109
  98.4 140.2 %all-gather.15.cloned.1.call-start = ((), (), s32[]{:S(2)}) async-start(), calls=%async_computation.5 | async-start | bytes 2433024 | tf_op jit(solution)/shard_map/all_gather | solution.py:159
  113.2 53.4 %copy-start.3 = (bf16[33,28,256]{2,1,0:T(8,128)(2,1)S(1)}, bf16[33,28,256]{2,1,0:T(8,128)(2,1)}, u32[]{:S(2)}) copy-start(bf16[33,28,256]{2,1,0:T(8,128)(2,1)} %slice.146) | copy-start | bytes 1419268
  196.9 1.0 copy-start.1
  198.7 1.4 copy-start.5
  200.7 5.2 %copy-start.7 = (bf16[9,128]{1,0:T(8,128)(2,1)S(1)}, bf16[9,128]{1,0:T(8,128)(2,1)}, u32[]{:S(2)}) copy-start(bf16[9,128]{1,0:T(8,128)(2,1)} %param.28) | copy-start | bytes 6916
  204.9 80.7 %all-gather.17.cloned.1.call-start = ((), (), s32[]{:S(2)}) async-start(), calls=%async_computation.6 | async-start | bytes 2433024 | tf_op jit(solution)/shard_map/all_gather | solution.py:186
  205.9 4.1 %slice-start = ((bf16[32,74,256]{2,0,1:T(8,128)(2,1)}), bf16[32,4,256]{2,0,1:T(8,128)(2,1)S(1)}, s32[]{:S(2)}) async-start(bf16[32,74,256]{2,0,1:T(8,128)(2,1)} %copy-done.1), calls=%async_computation.7 | async-start | bytes 131072 | tf_op jit(solution)/shard_map/slice | solution.py:134
  242.3 5.7 %copy-start.4 = (bf16[1024,2,128]{2,1,0:T(2,128)(2,1)S(1)}, bf16[1024,2,128]{2,1,0:T(2,128)(2,1)}, u32[]{:S(2)}) copy-start(bf16[1024,2,128]{2,1,0:T(2,128)(2,1)} %param.27) | copy-start | bytes 1572868
  242.3 5.7 %copy-start.9 = (f32[1024]{0:T(1024)S(1)}, f32[1024]{0:T(1024)}, u32[]{:S(2)}) copy-start(f32[1024]{0:T(1024)} %param.26) | copy-start | bytes 12292
  247.9 1.8 copy-start.2
  249.8 0.7 copy-start.11
  249.8 0.7 copy-start.12
Sparse Core Ops, SparseCore 0:
  66.4 28.7 all-gather.12
  97.8 33.4 all-gather.8
  133.4 33.2 all-gather.10
  205.0 33.4 all-gather.14
  252.0 33.5 all-gather.16

commit v6 on v1

--- a/solution.py
+++ b/solution.py
@@ -102,6 +102,10 @@
         preferred_element_type=jnp.float32,
     ).astype(jnp.bfloat16)
 
+    out_span = frame_span
+    frame_span = -(-frame_span // 16) * 16
+    arranged = jnp.pad(arranged, ((0, 0), (0, frame_span - out_span), (0, 0)))
+
     x_all = lax.all_gather(arranged, "ingest", axis=0, tiled=False)
     w_out_in, w_pw2_in, x_all = lax.optimization_barrier((w_out, w_pw2, x_all))
     w_out_full = lax.all_gather(w_out_in, "ingest", axis=0, tiled=True)
@@ -194,6 +198,7 @@
     result = (residual_own + conv_terms).reshape(utterances, frame_span, local_width)
     live_rows = frame_index[None, :] < frames[:, None]
     layer_out = jnp.where(live_rows[:, :, None], result, 0.0).astype(jnp.bfloat16)
+    layer_out = layer_out[:, :out_span]
 
     keep = jnp.arange(cache_len, dtype=jnp.int32)
     kv_pick = position[None, None, :] == keep[None, :, None] + frames[:, None, None]

time: 295 us -> 289 us (0.980)
  local copies, waits for them, and re-layouts: 32.4 us -> 22.9 us
  waiting for transfers between devices: 185 us -> 189 us
    all_gather x1, waiting for transfers between devices: 20.3 us -> 28 us  [shards(): w_out_full = lax.all_gather(w_out_in, 'ingest', axis=0, tiled=True)]
    convert_element_type x3 -> x0, local copies, waits for them, and re-layouts: 6.5 us -> none  [the longest x2 5.75 us: normalize(): ((values - row_mean) * lax.rsqrt(spread + norm_eps) * gain_cols).astype(j...]
    convert_element_type x1, local copies, waits for them, and re-layouts: 0.72 us -> 5.92 us  [shards(): x_rows = x_rows.astype(jnp.float32)]
    reshape x4 -> x0, local copies, waits for them, and re-layouts: 5.1 us -> none  [the longest x1 2.54 us: shards(): act_all.reshape(groups, row_count, local_width)]
    all_gather x1, waiting for transfers between devices: 28.9 us -> 25.1 us  [shards(): ctx_all = lax.all_gather(context, 'ingest', axis=0, tiled=False)]
    unnamed x34 -> x33, local copies, waits for them, and re-layouts: 7.27 us -> 4.01 us
  transfers between devices with their start and end apart: 7 -> 7, of which waited for: 7 -> 7; matrix products, arithmetic and copies ran while one was open for 10% -> 9% of each run, Pallas kernels for 0% -> 0%
where the time goes in v6:
time: 289 us; the launch traced here: 288 us
  waiting for transfers between devices  189 us (65%)
  starting transfers between devices  28.5 us (10%)
  local copies, waits for them, and re-layouts  22.9 us (8%)
  matrix products  21.7 us (8%)
  between operations  14.2 us (5%)
  other arithmetic  11.9 us (4%)
    all_gather x1, waiting for transfers between devices, shards(): w_pw2_full = lax.all_gather(w_pw2_in, 'ingest', axis=0, tiled=True)  35.4 us
    all_gather x1, waiting for transfers between devices, shards(): act_all = lax.all_gather(activated, 'ingest', axis=0, tiled=False)  29.6 us
    all_to_all x1, waiting for transfers between devices, shards(): lax.all_to_all(frame_send, 'owner', split_axis=0, concat_axis=0, tiled=True)  29.3 us
    all_gather x1, waiting for transfers between devices, shards(): w_out_full = lax.all_gather(w_out_in, 'ingest', axis=0, tiled=True)  28 us
    all_to_all x1, waiting for transfers between devices, shards(): lax.all_to_all(cache_send, 'owner', split_axis=0, concat_axis=0, tiled=True)  25.6 us
    all_gather x1, waiting for transfers between devices, shards(): ctx_all = lax.all_gather(context, 'ingest', axis=0, tiled=False)  25.1 us
    all_to_all x1, starting transfers between devices, shards(): lax.all_to_all(frame_send, 'owner', split_axis=0, concat_axis=0, tiled=True)  19.1 us
    all_gather x1, waiting for transfers between devices, shards(): x_all = lax.all_gather(arranged, 'ingest', axis=0, tiled=False)  15.3 us
  transfers between devices with their start and end apart: 7, of which 7 were waited for; matrix products, arithmetic and copies ran while one was open for 9% of the time, Pallas kernels for 0%

profile of v6, /device:TPU:1, one launch (start us, length us, event | category | flops | bytes accessed | tf_op | source)
XLA Modules:
  0.0 288.1 jit_solution(5876220783078511619)
XLA Ops:
  10.2 1.1 copy.54
  11.4 19.1 %all-to-all-start = ((bf16[64,32,128]{2,1,0:T(8,128)(2,1)}), bf16[64,32,128]{2,1,0:T(8,128)(2,1)S(1)}, u32[]{:S(2)}, u32[]{:S(2)}) async-start(bf16[64,32,128]{2,1,0:T(8,128)(2,1)} %copy.54), calls=%async_computation | async-start | bytes 1048576 | tf_op jit(solution)/shard_map/all_to_all | solution.py:69
  30.5 29.3 %all-to-all-done = bf16[64,32,128]{2,1,0:T(8,128)(2,1)S(1)} async-done(((bf16[64,32,128]{2,1,0:T(8,128)(2,1)}), bf16[64,32,128]{2,1,0:T(8,128)(2,1)S(1)}, u32[]{:S(2)}, u32[]{:S(2)}) %all-to-all-start) | async-done | bytes 524320 | tf_op jit(solution)/shard_map/all_to_all | solution.py:69
  59.9 1.2 fusion.70
  64.1 3.0 %copy.61 = bf16[64,80,256]{2,1,0:T(8,128)(2,1)} copy(bf16[64,80,256]{2,0,1:T(8,128)(2,1)S(1)} %convolution_convert_fusion) | data formatting | bytes 5242880 | tf_op jit(solution)/shard_map/convert_element_type | solution.py:93
  67.1 8.8 %all-to-all-start.1 = ((bf16[64,80,256]{2,1,0:T(8,128)(2,1)}), bf16[64,80,256]{2,1,0:T(8,128)(2,1)S(1)}, u32[]{:S(2)}, u32[]{:S(2)}) async-start(bf16[64,80,256]{2,1,0:T(8,128)(2,1)} %copy.61), calls=%async_computation.1 | async-start | bytes 5242880 | tf_op jit(solution)/shard_map/all_to_all | solution.py:94
  75.9 15.3 %all-gather.13.cloned.1.call-done = bf16[264,32,128]{2,1,0:T(8,128)(2,1)} async-done(((bf16[33,32,128]{2,1,0:T(8,128)(2,1)}), bf16[264,32,128]{2,1,0:T(8,128)(2,1)}) %all-gather.13.cloned.1.call-update) | async-done | bytes 2162704 | tf_op jit(solution)/shard_map/all_gather | solution.py:109
  93.4 2.5 fusion.1
  95.9 1.4 fusion.24
  98.8 28.0 %all-gather.9.cloned.1.call-done = bf16[1024,1024]{1,0:T(8,128)(2,1)} async-done(((bf16[128,1024]{1,0:T(8,128)(2,1)}), bf16[1024,1024]{1,0:T(8,128)(2,1)}) %all-gather.9.cloned.1.call-update) | async-done | bytes 2097168 | tf_op jit(solution)/shard_map/all_gather | solution.py:111
  126.8 35.4 %all-gather.11.cloned.1.call-done = bf16[1024,1024]{1,0:T(8,128)(2,1)} async-done(((bf16[128,1024]{1,0:T(8,128)(2,1)}), bf16[1024,1024]{1,0:T(8,128)(2,1)}) %all-gather.11.cloned.1.call-update) | async-done | bytes 2097168 | tf_op jit(solution)/shard_map/all_gather | solution.py:112
  162.2 2.2 copy.64
  164.4 25.6 %all-to-all-done.1 = bf16[64,80,256]{2,1,0:T(8,128)(2,1)S(1)} async-done(((bf16[64,80,256]{2,1,0:T(8,128)(2,1)}), bf16[64,80,256]{2,1,0:T(8,128)(2,1)S(1)}, u32[]{:S(2)}, u32[]{:S(2)}) %all-to-all-start.1) | async-done | bytes 2621472 | tf_op jit(solution)/shard_map/all_to_all | solution.py:94
  190.0 1.2 fusion.69
  194.0 1.4 fusion.91
  196.3 3.8 %convolution_convert_fusion.3 = bf16[33,32,128]{2,1,0:T(8,128)(2,1)} fusion(bf16[33,102,128]{2,0,1:T(8,128)(2,1)} %get-tuple-element.34, f32[33,32]{1,0:T(8,128)S(1)} %fusion.92, f32[33,32,102]{2,1,0:T(8,128)S(1)} %fusion.35), kind=kOutput, calls=%fused_computation.41 | convolution fusion | flops 28033732 | bytes 1567104 | tf_op jit(solution)/shard_map/sqk,skd->sqd/dot_general | solution.py:159
  200.5 2.2 convert_bitcast_fusion
  202.7 5.9 %copy.57 = f32[33,32,8,128]{3,2,1,0:T(8,128)} copy(f32[33,32,8,128]{3,1,0,2:T(8,128)S(1)} %convert_bitcast_fusion) | data formatting | bytes 8650752 | tf_op jit(solution)/shard_map/convert_element_type | solution.py:114
  208.7 25.1 %all-gather.15.cloned.1.call-done = bf16[264,32,128]{2,1,0:T(8,128)(2,1)} async-done(((bf16[33,32,128]{2,1,0:T(8,128)(2,1)}), bf16[264,32,128]{2,1,0:T(8,128)(2,1)}) %all-gather.15.cloned.1.call-update) | async-done | bytes 2162704 | tf_op jit(solution)/shard_map/all_gather | solution.py:163
  233.8 6.6 %fusion.90 = (f32[1056]{0:T(1024)S(1)}, f32[1056]{0:T(1024)S(1)}, f32[1056,1024]{1,0:T(8,128)S(1)}) fusion(bf16[8,1056,128]{2,1,0:T(8,128)(2,1)} %bitcast.119, bf16[8,128,1024]{2,1,0:T(8,128)(2,1)} %bitcast.120, f32[132,8,8,128]{3,2,1,0:T(8,128)} %bitcast.111), kind=kOutput, calls=%fused_computation.145 | convolution fusion | flops 2218915840 | bytes 12919040 | tf_op jit(solution)/shard_map/grc,gcn->rn/dot_general | solution.py:165
  243.1 1.4 multiply_convert_fusion.3
  245.7 2.0 fusion.21
  248.6 29.6 %all-gather.17.cloned.1.call-done = bf16[264,32,128]{2,1,0:T(8,128)(2,1)} async-done(((bf16[33,32,128]{2,1,0:T(8,128)(2,1)}), bf16[264,32,128]{2,1,0:T(8,128)(2,1)}) %all-gather.17.cloned.1.call-update) | async-done | bytes 2162704 | tf_op jit(solution)/shard_map/all_gather | solution.py:190
  278.3 2.4 fusion.2
  (92 shorter events, 19.4 us)
Async XLA Ops:
  7.2 88.7 %copy-start = (bf16[1024,1,384]{2,0,1:T(8,128)(2,1)S(1)}, bf16[1024,1,384]{2,0,1:T(8,128)(2,1)}, u32[]{:S(2)}) copy-start(bf16[1024,1,384]{2,0,1:T(8,128)(2,1)} %param.24) | copy-start | bytes 2359300
  10.2 52.1 %slice-start.2 = ((bf16[33,8,128]{2,1,0:T(8,128)(2,1)}), bf16[32,8,128]{2,1,0:T(8,128)(2,1)S(1)}, s32[]{:S(2)}) async-start(bf16[33,8,128]{2,1,0:T(8,128)(2,1)} %param.21), calls=%async_computation.9 | async-start | bytes 131072 | tf_op jit(solution)/shard_map/slice | solution.py:82
  11.4 48.5 %all-to-all-start = ((bf16[64,32,128]{2,1,0:T(8,128)(2,1)}), bf16[64,32,128]{2,1,0:T(8,128)(2,1)S(1)}, u32[]{:S(2)}, u32[]{:S(2)}) async-start(bf16[64,32,128]{2,1,0:T(8,128)(2,1)} %copy.54), calls=%async_computation | async-start | bytes 1048576 | tf_op jit(solution)/shard_map/all_to_all | solution.py:69
  30.5 60.7 %all-gather.13.cloned.1.call-start = ((), (), s32[]{:S(2)}) async-start(), calls=%async_computation.4 | async-start | bytes 2433024 | tf_op jit(solution)/shard_map/all_gather | solution.py:109
  61.4 1.4 slice-start.1
  62.4 0.7 copy-start.11
  67.1 26.2 %copy-start.8 = (s32[33]{0:T(128)S(1)}, s32[33]{0:T(128)}, u32[]{:S(2)}) copy-start(s32[33]{0:T(128)} %param.19) | copy-start | bytes 400
  67.1 123.0 %all-to-all-start.1 = ((bf16[64,80,256]{2,1,0:T(8,128)(2,1)}), bf16[64,80,256]{2,1,0:T(8,128)(2,1)S(1)}, u32[]{:S(2)}, u32[]{:S(2)}) async-start(bf16[64,80,256]{2,1,0:T(8,128)(2,1)} %copy.61), calls=%async_computation.1 | async-start | bytes 5242880 | tf_op jit(solution)/shard_map/all_to_all | solution.py:94
  75.9 20.0 %copy-start.14 = (f32[1024]{0:T(1024)S(1)}, f32[1024]{0:T(1024)}, u32[]{:S(2)}) copy-start(f32[1024]{0:T(1024)} %param.23) | copy-start | bytes 12292
  75.9 50.9 %all-gather.9.cloned.1.call-start = ((), (), s32[]{:S(2)}) async-start(), calls=%async_computation.2 | async-start | bytes 2359296 | tf_op jit(solution)/shard_map/all_gather | solution.py:111
  91.2 71.0 %all-gather.11.cloned.1.call-start = ((), (), s32[]{:S(2)}) async-start(), calls=%async_computation.3 | async-start | bytes 2359296 | tf_op jit(solution)/shard_map/all_gather | solution.py:112
  92.0 141.9 %all-gather.15.cloned.1.call-start = ((), (), s32[]{:S(2)}) async-start(), calls=%async_computation.5 | async-start | bytes 2433024 | tf_op jit(solution)/shard_map/all_gather | solution.py:163
  92.2 3.7 %copy-start.1 = (bf16[264,32,128]{2,1,0:T(8,128)(2,1)S(1)}, bf16[264,32,128]{2,1,0:T(8,128)(2,1)}, u32[]{:S(2)}) copy-start(bf16[264,32,128]{2,1,0:T(8,128)(2,1)} %all-gather.13.cloned.1.call-done) | copy-start | bytes 6488068
  191.3 1.9 copy-start.4
  192.1 1.0 copy-start.3
  194.0 1.4 copy-start.6
  195.9 4.5 %copy-start.7 = (bf16[33,8,128]{2,1,0:T(8,128)(2,1)S(1)}, bf16[33,8,128]{2,1,0:T(8,128)(2,1)}, u32[]{:S(2)}) copy-start(bf16[33,8,128]{2,1,0:T(8,128)(2,1)} %param.21) | copy-start | bytes 202756
  195.9 4.5 %copy-start.9 = (bf16[9,128]{1,0:T(8,128)(2,1)S(1)}, bf16[9,128]{1,0:T(8,128)(2,1)}, u32[]{:S(2)}) copy-start(bf16[9,128]{1,0:T(8,128)(2,1)} %param.28) | copy-start | bytes 6916
  200.2 78.1 %all-gather.17.cloned.1.call-start = ((), (), s32[]{:S(2)}) async-start(), calls=%async_computation.6 | async-start | bytes 2433024 | tf_op jit(solution)/shard_map/all_gather | solution.py:190
  202.7 5.9 %slice-start = ((bf16[32,74,256]{2,0,1:T(8,128)(2,1)}), bf16[32,4,256]{2,0,1:T(8,128)(2,1)S(1)}, s32[]{:S(2)}) async-start(bf16[32,74,256]{2,0,1:T(8,128)(2,1)} %copy-done.3), calls=%async_computation.7 | async-start | bytes 131072 | tf_op jit(solution)/shard_map/slice | solution.py:138
  233.8 6.6 %copy-start.5 = (bf16[1024,2,128]{2,1,0:T(2,128)(2,1)S(1)}, bf16[1024,2,128]{2,1,0:T(2,128)(2,1)}, u32[]{:S(2)}) copy-start(bf16[1024,2,128]{2,1,0:T(2,128)(2,1)} %param.27) | copy-start | bytes 1572868
  233.8 6.7 %copy-start.10 = (f32[1024]{0:T(1024)S(1)}, f32[1024]{0:T(1024)}, u32[]{:S(2)}) copy-start(f32[1024]{0:T(1024)} %param.26) | copy-start | bytes 12292
  240.4 2.0 copy-start.2
  242.4 0.7 copy-start.13
  (1 other events, 0.7 us)
Sparse Core Ops, SparseCore 0:
  62.4 28.7 all-gather.12
  93.3 33.4 all-gather.8
  129.0 33.2 all-gather.10
  200.3 33.4 all-gather.14
  244.7 33.5 all-gather.16

commit v7 on v5

--- a/solution.py
+++ b/solution.py
@@ -66,6 +66,7 @@
         frame_rows_tagged,
         preferred_element_type=jnp.float32,
     ).astype(jnp.bfloat16)
+    frame_got = lax.all_to_all(frame_send, "owner", split_axis=0, concat_axis=0, tiled=True)
 
     kv_lanes = 2 * head_dim
     conv_fold = conv_len * local_width // kv_lanes
@@ -90,8 +91,6 @@
         cache_rows,
         preferred_element_type=jnp.float32,
     ).astype(jnp.bfloat16)
-    frame_send = frame_send + 0 * cache_send[:, : frame_send.shape[1], : frame_send.shape[2]]
-    frame_got = lax.all_to_all(frame_send, "owner", split_axis=0, concat_axis=0, tiled=True)
     cache_got = lax.all_to_all(cache_send, "owner", split_axis=0, concat_axis=0, tiled=True)
 
     got_slot = frame_got[:, frame_span, 0].astype(jnp.int32)
@@ -102,6 +101,10 @@
         frame_got[:, :frame_span],
         preferred_element_type=jnp.float32,
     ).astype(jnp.bfloat16)
+
+    out_span = frame_span
+    frame_span = -(-frame_span // 16) * 16
+    arranged = jnp.pad(arranged, ((0, 0), (0, frame_span - out_span), (0, 0)))
 
     x_all = lax.all_gather(arranged, "ingest", axis=0, tiled=False)
     w_out_in, w_pw2_in, x_all = lax.optimization_barrier((w_out, w_pw2, x_all))
@@ -194,6 +197,7 @@
     result = (residual_own + conv_terms).reshape(utterances, frame_span, local_width)
     live_rows = frame_index[None, :] < frames[:, None]
     layer_out = jnp.where(live_rows[:, :, None], result, 0.0).astype(jnp.bfloat16)
+    layer_out = layer_out[:, :out_span]
 
     keep = jnp.arange(cache_len, dtype=jnp.int32)
     kv_pick = position[None, None, :] == keep[None, :, None] + frames[:, None, None]

time: 298 us -> 288 us (0.966)
  local copies, waits for them, and re-layouts: 40.5 us -> 18.7 us
  waiting for transfers between devices: 179 us -> 195 us
    all_gather x1, waiting for transfers between devices: 13.8 us -> 26.3 us  [shards(): w_out_full = lax.all_gather(w_out_in, 'ingest', axis=0, tiled=True)]
    convert_element_type x4 -> x1, local copies, waits for them, and re-layouts: 10.6 us -> 1.14 us  [shards(): frame_send = jnp.einsum('ds,stc->dtc', (dest[:, None] == route_owner[None...]
    reshape x4 -> x0, local copies, waits for them, and re-layouts: 6.25 us -> none  [the longest x1 3.69 us: shards(): ctx_all.reshape(groups, row_count, head_dim)]
    all_gather x1, waiting for transfers between devices: 28.5 us -> 32.3 us  [shards(): ctx_all = lax.all_gather(context, 'ingest', axis=0, tiled=False)]
  transfers between devices with their start and end apart: 7 -> 7, of which waited for: 7 -> 7; matrix products, arithmetic and copies ran while one was open for 11% -> 7% of each run, Pallas kernels for 0% -> 0%
where the time goes in v7:
time: 288 us
  waiting for transfers between devices  195 us (68%)
  starting transfers between devices  28.5 us (10%)
  matrix products  20.8 us (7%)
  local copies, waits for them, and re-layouts  18.7 us (6%)
  between operations  14.1 us (5%)
  other arithmetic  11.3 us (4%)
    all_gather x1, waiting for transfers between devices, shards(): w_pw2_full = lax.all_gather(w_pw2_in, 'ingest', axis=0, tiled=True)  35.4 us
    all_gather x1, waiting for transfers between devices, shards(): ctx_all = lax.all_gather(context, 'ingest', axis=0, tiled=False)  32.3 us
    all_gather x1, waiting for transfers between devices, shards(): act_all = lax.all_gather(activated, 'ingest', axis=0, tiled=False)  29.6 us
    all_to_all x1, waiting for transfers between devices, shards(): lax.all_to_all(frame_send, 'owner', split_axis=0, concat_axis=0, tiled=True)  29.3 us
    all_gather x1, waiting for transfers between devices, shards(): w_out_full = lax.all_gather(w_out_in, 'ingest', axis=0, tiled=True)  26.3 us
    all_to_all x1, waiting for transfers between devices, shards(): lax.all_to_all(cache_send, 'owner', split_axis=0, concat_axis=0, tiled=True)  25.6 us
    all_to_all x1, starting transfers between devices, shards(): lax.all_to_all(frame_send, 'owner', split_axis=0, concat_axis=0, tiled=True)  19.1 us
    all_gather x1, waiting for transfers between devices, shards(): x_all = lax.all_gather(arranged, 'ingest', axis=0, tiled=False)  15.2 us
  transfers between devices with their start and end apart: 7, of which 7 were waited for; matrix products, arithmetic and copies ran while one was open for 7% of the time, Pallas kernels for 0%

profile of v7, /device:TPU:1, one launch (start us, length us, event | category | flops | bytes accessed | tf_op | source)
XLA Modules:
  0.0 287.9 jit_solution(12827155608465658466)
XLA Ops:
  10.2 1.1 copy.53
  11.4 19.1 %all-to-all-start = ((bf16[64,32,128]{2,1,0:T(8,128)(2,1)}), bf16[64,32,128]{2,1,0:T(8,128)(2,1)S(1)}, u32[]{:S(2)}, u32[]{:S(2)}) async-start(bf16[64,32,128]{2,1,0:T(8,128)(2,1)} %copy.53), calls=%async_computation | async-start | bytes 1048576 | tf_op jit(solution)/shard_map/all_to_all | solution.py:69
  30.5 29.3 %all-to-all-done = bf16[64,32,128]{2,1,0:T(8,128)(2,1)S(1)} async-done(((bf16[64,32,128]{2,1,0:T(8,128)(2,1)}), bf16[64,32,128]{2,1,0:T(8,128)(2,1)S(1)}, u32[]{:S(2)}, u32[]{:S(2)}) %all-to-all-start) | async-done | bytes 524320 | tf_op jit(solution)/shard_map/all_to_all | solution.py:69
  59.9 1.2 fusion.73
  64.1 3.0 %copy.60 = bf16[64,80,256]{2,1,0:T(8,128)(2,1)} copy(bf16[64,80,256]{2,0,1:T(8,128)(2,1)S(1)} %convolution_convert_fusion) | data formatting | bytes 5242880 | tf_op jit(solution)/shard_map/convert_element_type | solution.py:93
  67.1 8.8 %all-to-all-start.1 = ((bf16[64,80,256]{2,1,0:T(8,128)(2,1)}), bf16[64,80,256]{2,1,0:T(8,128)(2,1)S(1)}, u32[]{:S(2)}, u32[]{:S(2)}) async-start(bf16[64,80,256]{2,1,0:T(8,128)(2,1)} %copy.60), calls=%async_computation.1 | async-start | bytes 5242880 | tf_op jit(solution)/shard_map/all_to_all | solution.py:94
  76.0 15.2 %all-gather.13.cloned.1.call-done = bf16[264,32,128]{2,1,0:T(8,128)(2,1)} async-done(((bf16[33,32,128]{2,1,0:T(8,128)(2,1)}), bf16[264,32,128]{2,1,0:T(8,128)(2,1)}) %all-gather.13.cloned.1.call-update) | async-done | bytes 2162704 | tf_op jit(solution)/shard_map/all_gather | solution.py:109
  93.3 2.5 convert_reduce_fusion
  95.9 1.4 fusion.27
  98.9 1.7 copy_bitcast_fusion
  100.5 26.3 %all-gather.9.cloned.1.call-done = bf16[1024,1024]{1,0:T(8,128)(2,1)} async-done(((bf16[128,1024]{1,0:T(8,128)(2,1)}), bf16[1024,1024]{1,0:T(8,128)(2,1)}) %all-gather.9.cloned.1.call-update) | async-done | bytes 2097168 | tf_op jit(solution)/shard_map/all_gather | solution.py:111
  126.8 35.4 %all-gather.11.cloned.1.call-done = bf16[1024,1024]{1,0:T(8,128)(2,1)} async-done(((bf16[128,1024]{1,0:T(8,128)(2,1)}), bf16[1024,1024]{1,0:T(8,128)(2,1)}) %all-gather.11.cloned.1.call-update) | async-done | bytes 2097168 | tf_op jit(solution)/shard_map/all_gather | solution.py:112
  162.2 2.2 copy.63
  164.4 25.6 %all-to-all-done.1 = bf16[64,80,256]{2,1,0:T(8,128)(2,1)S(1)} async-done(((bf16[64,80,256]{2,1,0:T(8,128)(2,1)}), bf16[64,80,256]{2,1,0:T(8,128)(2,1)S(1)}, u32[]{:S(2)}, u32[]{:S(2)}) %all-to-all-start.1) | async-done | bytes 2621472 | tf_op jit(solution)/shard_map/all_to_all | solution.py:94
  190.1 1.2 fusion.72
  194.0 1.3 fusion.94
  196.9 3.8 %convolution_convert_fusion.3 = bf16[33,32,128]{2,1,0:T(8,128)(2,1)} fusion(bf16[33,102,128]{2,0,1:T(8,128)(2,1)} %get-tuple-element.36, f32[33,32]{1,0:T(8,128)} %fusion.95, f32[33,32,102]{2,1,0:T(8,128)S(1)} %fusion.38), kind=kOutput, calls=%fused_computation.45 | convolution fusion | flops 28033732 | bytes 1567104 | tf_op jit(solution)/shard_map/sqk,skd->sqd/dot_general | solution.py:158
  202.2 32.3 %all-gather.15.cloned.1.call-done = bf16[264,32,128]{2,1,0:T(8,128)(2,1)} async-done(((bf16[33,32,128]{2,1,0:T(8,128)(2,1)}), bf16[264,32,128]{2,1,0:T(8,128)(2,1)}) %all-gather.15.cloned.1.call-update) | async-done | bytes 2162704 | tf_op jit(solution)/shard_map/all_gather | solution.py:162
  234.5 5.7 %fusion.93 = (f32[1056]{0:T(1024)S(1)}, f32[1056]{0:T(1024)S(1)}, f32[1056,1024]{1,0:T(8,128)S(1)}) fusion(bf16[8,1056,128]{2,1,0:T(8,128)(2,1)} %bitcast.116, bf16[8,128,1024]{2,1,0:T(8,128)(2,1)} %bitcast.117, bf16[1056,1024]{1,0:T(8,128)(2,1)} %bitcast.109), kind=kOutput, calls=%fused_computation.149 | convolution fusion | flops 2219997184 | bytes 10756352 | tf_op jit(solution)/shard_map/grc,gcn->rn/dot_general | solution.py:164
  241.0 1.2 copy-done.2
  242.9 1.4 multiply_convert_fusion.2
  245.5 2.0 fusion.24
  248.4 29.6 %all-gather.17.cloned.1.call-done = bf16[264,32,128]{2,1,0:T(8,128)(2,1)} async-done(((bf16[33,32,128]{2,1,0:T(8,128)(2,1)}), bf16[264,32,128]{2,1,0:T(8,128)(2,1)}) %all-gather.17.cloned.1.call-update) | async-done | bytes 2162704 | tf_op jit(solution)/shard_map/all_gather | solution.py:189
  278.0 2.4 fusion.5
  (91 shorter events, 19.9 us)
Async XLA Ops:
  7.2 88.7 %copy-start = (bf16[1024,1,384]{2,0,1:T(8,128)(2,1)S(1)}, bf16[1024,1,384]{2,0,1:T(8,128)(2,1)}, u32[]{:S(2)}) copy-start(bf16[1024,1,384]{2,0,1:T(8,128)(2,1)} %param.24) | copy-start | bytes 2359300
  10.2 52.1 %slice-start.2 = ((bf16[33,8,128]{2,1,0:T(8,128)(2,1)}), bf16[32,8,128]{2,1,0:T(8,128)(2,1)S(1)}, s32[]{:S(2)}) async-start(bf16[33,8,128]{2,1,0:T(8,128)(2,1)} %param.21), calls=%async_computation.9 | async-start | bytes 131072 | tf_op jit(solution)/shard_map/slice | solution.py:82
  11.4 48.5 %all-to-all-start = ((bf16[64,32,128]{2,1,0:T(8,128)(2,1)}), bf16[64,32,128]{2,1,0:T(8,128)(2,1)S(1)}, u32[]{:S(2)}, u32[]{:S(2)}) async-start(bf16[64,32,128]{2,1,0:T(8,128)(2,1)} %copy.53), calls=%async_computation | async-start | bytes 1048576 | tf_op jit(solution)/shard_map/all_to_all | solution.py:69
  30.5 60.7 %all-gather.13.cloned.1.call-start = ((), (), s32[]{:S(2)}) async-start(), calls=%async_computation.4 | async-start | bytes 2433024 | tf_op jit(solution)/shard_map/all_gather | solution.py:109
  61.4 1.4 slice-start.1
  62.4 0.7 copy-start.11
  67.1 26.1 %copy-start.8 = (s32[33]{0:T(128)S(1)}, s32[33]{0:T(128)}, u32[]{:S(2)}) copy-start(s32[33]{0:T(128)} %param.19) | copy-start | bytes 400
  67.1 122.9 %all-to-all-start.1 = ((bf16[64,80,256]{2,1,0:T(8,128)(2,1)}), bf16[64,80,256]{2,1,0:T(8,128)(2,1)S(1)}, u32[]{:S(2)}, u32[]{:S(2)}) async-start(bf16[64,80,256]{2,1,0:T(8,128)(2,1)} %copy.60), calls=%async_computation.1 | async-start | bytes 5242880 | tf_op jit(solution)/shard_map/all_to_all | solution.py:94
  75.9 19.9 %copy-start.14 = (f32[1024]{0:T(1024)S(1)}, f32[1024]{0:T(1024)}, u32[]{:S(2)}) copy-start(f32[1024]{0:T(1024)} %param.23) | copy-start | bytes 12292
  75.9 50.9 %all-gather.9.cloned.1.call-start = ((), (), s32[]{:S(2)}) async-start(), calls=%async_computation.2 | async-start | bytes 2359296 | tf_op jit(solution)/shard_map/all_gather | solution.py:111
  91.2 71.0 %all-gather.11.cloned.1.call-start = ((), (), s32[]{:S(2)}) async-start(), calls=%async_computation.3 | async-start | bytes 2359296 | tf_op jit(solution)/shard_map/all_gather | solution.py:112
  91.9 142.5 %all-gather.15.cloned.1.call-start = ((), (), s32[]{:S(2)}) async-start(), calls=%async_computation.5 | async-start | bytes 2433024 | tf_op jit(solution)/shard_map/all_gather | solution.py:162
  92.2 3.7 %copy-start.1 = (bf16[264,32,128]{2,1,0:T(8,128)(2,1)S(1)}, bf16[264,32,128]{2,1,0:T(8,128)(2,1)}, u32[]{:S(2)}) copy-start(bf16[264,32,128]{2,1,0:T(8,128)(2,1)} %all-gather.13.cloned.1.call-done) | copy-start | bytes 6488068
  191.3 1.9 copy-start.4
  192.1 1.0 copy-start.3
  194.0 1.3 copy-start.6
  196.0 5.1 %copy-start.7 = (bf16[33,8,128]{2,1,0:T(8,128)(2,1)S(1)}, bf16[33,8,128]{2,1,0:T(8,128)(2,1)}, u32[]{:S(2)}) copy-start(bf16[33,8,128]{2,1,0:T(8,128)(2,1)} %param.21) | copy-start | bytes 202756
  196.0 6.1 %slice-start = ((bf16[32,74,256]{2,0,1:T(8,128)(2,1)}), bf16[32,4,256]{2,0,1:T(8,128)(2,1)S(1)}, s32[]{:S(2)}) async-start(bf16[32,74,256]{2,0,1:T(8,128)(2,1)} %copy-done.3), calls=%async_computation.7 | async-start | bytes 131072 | tf_op jit(solution)/shard_map/slice | solution.py:137
  200.8 77.2 %all-gather.17.cloned.1.call-start = ((), (), s32[]{:S(2)}) async-start(), calls=%async_computation.6 | async-start | bytes 2433024 | tf_op jit(solution)/shard_map/all_gather | solution.py:189
  234.5 5.7 %copy-start.5 = (bf16[1024,2,128]{2,1,0:T(2,128)(2,1)S(1)}, bf16[1024,2,128]{2,1,0:T(2,128)(2,1)}, u32[]{:S(2)}) copy-start(bf16[1024,2,128]{2,1,0:T(2,128)(2,1)} %param.27) | copy-start | bytes 1572868
  234.5 5.7 %copy-start.10 = (f32[1024]{0:T(1024)S(1)}, f32[1024]{0:T(1024)}, u32[]{:S(2)}) copy-start(f32[1024]{0:T(1024)} %param.26) | copy-start | bytes 12292
  240.1 2.1 copy-start.2
  242.2 0.7 copy-start.13
  242.9 1.4 copy-start.9
  (1 other events, 0.7 us)
Sparse Core Ops, SparseCore 0:
  62.4 28.7 all-gather.12
  93.3 33.4 all-gather.8
  129.0 33.2 all-gather.10
  200.9 33.4 all-gather.14
  244.4 33.5 all-gather.16

commit v8 on v6

--- a/solution.py
+++ b/solution.py
@@ -48,48 +48,49 @@
     settled = utterances - moving
 
     dest = jnp.arange(owners, dtype=jnp.int32)
-    frame_pad = -(-(frame_span + 1) // 16) * 16
+    frame_pad = -(-(frame_span + conv_len + 2) // 16) * 16
     slot_tag = jnp.broadcast_to(
         (route_slot + 1).astype(jnp.bfloat16)[:, None, None], (utterances, 1, local_width)
-    )
-    frame_rows_tagged = jnp.concatenate(
-        [
-            frame_rows,
-            slot_tag,
-            jnp.zeros((utterances, frame_pad - frame_span - 1, local_width), jnp.bfloat16),
-        ],
-        axis=1,
     )
     frame_send = jnp.einsum(
         "ds,stc->dtc",
         (dest[:, None] == route_owner[None, :]).astype(jnp.bfloat16),
-        frame_rows_tagged,
-        preferred_element_type=jnp.float32,
-    ).astype(jnp.bfloat16)
-    frame_got = lax.all_to_all(frame_send, "owner", split_axis=0, concat_axis=0, tiled=True)
-
-    kv_lanes = 2 * head_dim
-    conv_fold = conv_len * local_width // kv_lanes
-    cache_used = cache_len + conv_fold + 1
-    cache_pad = -(-cache_used // 16) * 16
+        jnp.concatenate([frame_rows, slot_tag], axis=1),
+        preferred_element_type=jnp.float32,
+    ).astype(jnp.bfloat16)
     mover_tag = jnp.broadcast_to(
         (jnp.arange(moving, dtype=jnp.int32) + 1).astype(jnp.bfloat16)[:, None, None],
-        (moving, 1, kv_lanes),
-    )
+        (moving, 1, local_width),
+    )
+    mig_pick = (dest[:, None] == mig_owner[None, :]).astype(jnp.bfloat16)
+    conv_send = jnp.einsum(
+        "dj,jrc->drc",
+        mig_pick,
+        jnp.concatenate([conv_cache[settled:], mover_tag], axis=1),
+        preferred_element_type=jnp.float32,
+    ).astype(jnp.bfloat16)
+    frame_send = jnp.concatenate(
+        [
+            frame_send,
+            conv_send,
+            jnp.zeros((owners, frame_pad - frame_span - conv_len - 2, local_width), jnp.bfloat16),
+        ],
+        axis=1,
+    )
+    frame_got = lax.all_to_all(frame_send, "owner", split_axis=0, concat_axis=0, tiled=True)
+
+    kv_lanes = 2 * head_dim
+    kv_rows = cache_len * kv_lanes // local_width
+    cache_pad = -(-kv_rows // 16) * 16
     cache_rows = jnp.concatenate(
         [
-            kv_cache[settled:, 0],
-            conv_cache[settled:].reshape(moving, conv_fold, kv_lanes),
-            mover_tag,
-            jnp.zeros((moving, cache_pad - cache_used, kv_lanes), jnp.bfloat16),
+            kv_cache[settled:, 0].reshape(moving, kv_rows, local_width),
+            jnp.zeros((moving, cache_pad - kv_rows, local_width), jnp.bfloat16),
         ],
         axis=1,
     )
     cache_send = jnp.einsum(
-        "dj,jrc->drc",
-        (dest[:, None] == mig_owner[None, :]).astype(jnp.bfloat16),
-        cache_rows,
-        preferred_element_type=jnp.float32,
+        "dj,jrc->drc", mig_pick, cache_rows, preferred_element_type=jnp.float32
     ).astype(jnp.bfloat16)
     cache_got = lax.all_to_all(cache_send, "owner", split_axis=0, concat_axis=0, tiled=True)
 
@@ -125,19 +126,22 @@
         groups, local_width, local_width
     )
 
-    got_mover = cache_got[:, cache_used - 1, 0].astype(jnp.int32)
+    got_mover = frame_got[:, out_span + 1 + conv_len, 0].astype(jnp.int32)
     movers = jnp.arange(moving, dtype=jnp.int32)
-    moved = jnp.einsum(
+    mover_from = (movers[:, None] + 1 == got_mover[None, :]).astype(jnp.bfloat16)
+    moved_kv = jnp.einsum(
+        "jo,orc->jrc", mover_from, cache_got[:, :kv_rows], preferred_element_type=jnp.float32
+    ).astype(jnp.bfloat16)
+    moved_conv = jnp.einsum(
         "jo,orc->jrc",
-        (movers[:, None] + 1 == got_mover[None, :]).astype(jnp.bfloat16),
-        cache_got[:, : cache_used - 1],
-        preferred_element_type=jnp.float32,
-    ).astype(jnp.bfloat16)
-    kv_state = jnp.concatenate([kv_cache[:settled, 0], moved[:, :cache_len]], axis=0)
-    conv_state = jnp.concatenate(
-        [conv_cache[:settled], moved[:, cache_len:].reshape(moving, conv_len, local_width)],
-        axis=0,
-    )
+        mover_from,
+        frame_got[:, out_span + 1 : out_span + 1 + conv_len],
+        preferred_element_type=jnp.float32,
+    ).astype(jnp.bfloat16)
+    kv_state = jnp.concatenate(
+        [kv_cache[:settled, 0], moved_kv.reshape(moving, cache_len, kv_lanes)], axis=0
+    )
+    conv_state = jnp.concatenate([conv_cache[:settled], moved_conv], axis=0)
 
     memory = jnp.concatenate([kv_state, fresh], axis=1)
     keys_total = memory.shape[1]

time: 289 us -> 290 us (level)
    all_to_all x1, waiting for transfers between devices: 25.6 us -> 79.5 us  [shards(): lax.all_to_all(cache_send, 'owner', split_axis=0, concat_axis=0, tiled=True)]
    all_gather x1, waiting for transfers between devices: 35.4 us -> 0.02 us  [shards(): w_pw2_full = lax.all_gather(w_pw2_in, 'ingest', axis=0, tiled=True)]
    all_gather x1, waiting for transfers between devices: 28 us -> 0.02 us  [shards(): w_out_full = lax.all_gather(w_out_in, 'ingest', axis=0, tiled=True)]
    all_to_all x1, waiting for transfers between devices: 29.3 us -> 39.7 us  [shards(): lax.all_to_all(frame_send, 'owner', split_axis=0, concat_axis=0, tiled=True)]
  transfers between devices with their start and end apart: 7 -> 7, of which waited for: 7 -> 5; matrix products, arithmetic and copies ran while one was open for 9% -> 9% of each run, Pallas kernels for 0% -> 0%
where the time goes in v8:
time: 290 us
  waiting for transfers between devices  189 us (65%)
  starting transfers between devices  29.3 us (10%)
  matrix products  22.6 us (8%)
  local copies, waits for them, and re-layouts  21.7 us (7%)
  between operations  14.3 us (5%)
  other arithmetic  13 us (4%)
    all_to_all x1, waiting for transfers between devices, shards(): lax.all_to_all(cache_send, 'owner', split_axis=0, concat_axis=0, tiled=True)  79.5 us
    all_to_all x1, waiting for transfers between devices, shards(): lax.all_to_all(frame_send, 'owner', split_axis=0, concat_axis=0, tiled=True)  39.7 us
    all_gather x1, waiting for transfers between devices, shards(): act_all = lax.all_gather(activated, 'ingest', axis=0, tiled=False)  29.7 us
    all_gather x1, waiting for transfers between devices, shards(): ctx_all = lax.all_gather(context, 'ingest', axis=0, tiled=False)  24.2 us
    all_to_all x1, starting transfers between devices, shards(): lax.all_to_all(frame_send, 'owner', split_axis=0, concat_axis=0, tiled=True)  19.1 us
    all_gather x1, waiting for transfers between devices, shards(): x_all = lax.all_gather(arranged, 'ingest', axis=0, tiled=False)  15 us
    all_to_all x1, starting transfers between devices, shards(): lax.all_to_all(cache_send, 'owner', split_axis=0, concat_axis=0, tiled=True)  9.58 us
    dot_general x1, matrix products, shards(): jnp.einsum('grc,gcn->rn', ctx_all.reshape(groups, row_count, head_dim), w...  6 us
  transfers between devices with their start and end apart: 7, of which 5 were waited for; matrix products, arithmetic and copies ran while one was open for 9% of the time, Pallas kernels for 0%

profile of v8, /device:TPU:1, one launch (start us, length us, event | category | flops | bytes accessed | tf_op | source)
XLA Modules:
  0.0 289.7 jit_solution(5278090643552473217)
XLA Ops:
  8.8 1.1 copy.44
  11.0 1.1 convolution_convert_fusion.2
  12.3 1.4 copy.46
  13.6 19.1 %all-to-all-start = ((bf16[64,48,128]{2,1,0:T(8,128)(2,1)}), bf16[64,48,128]{2,1,0:T(8,128)(2,1)S(1)}, u32[]{:S(2)}, u32[]{:S(2)}) async-start(bf16[64,48,128]{2,1,0:T(8,128)(2,1)} %copy.46), calls=%async_computation | async-start | bytes 1572864 | tf_op jit(solution)/shard_map/all_to_all | solution.py:80
  32.8 39.7 %all-to-all-done = bf16[64,48,128]{2,1,0:T(8,128)(2,1)S(1)} async-done(((bf16[64,48,128]{2,1,0:T(8,128)(2,1)}), bf16[64,48,128]{2,1,0:T(8,128)(2,1)S(1)}, u32[]{:S(2)}, u32[]{:S(2)}) %all-to-all-start) | async-done | bytes 786464 | tf_op jit(solution)/shard_map/all_to_all | solution.py:80
  72.6 2.4 fusion.58
  77.9 3.0 %copy.52 = bf16[64,144,128]{2,1,0:T(8,128)(2,1)} copy(bf16[64,144,128]{2,0,1:T(8,128)(2,1)S(1)} %convolution_convert_fusion) | data formatting | bytes 4718592 | tf_op jit(solution)/shard_map/convert_element_type | solution.py:94
  80.8 9.6 %all-to-all-start.1 = ((bf16[64,144,128]{2,1,0:T(8,128)(2,1)}), bf16[64,144,128]{2,1,0:T(8,128)(2,1)S(1)}, u32[]{:S(2)}, u32[]{:S(2)}) async-start(bf16[64,144,128]{2,1,0:T(8,128)(2,1)} %copy.52), calls=%async_computation.1 | async-start | bytes 4718592 | tf_op jit(solution)/shard_map/all_to_all | solution.py:95
  90.5 15.0 %all-gather.13.cloned.1.call-done = bf16[264,32,128]{2,1,0:T(8,128)(2,1)} async-done(((bf16[33,32,128]{2,1,0:T(8,128)(2,1)}), bf16[264,32,128]{2,1,0:T(8,128)(2,1)}) %all-gather.13.cloned.1.call-update) | async-done | bytes 2162704 | tf_op jit(solution)/shard_map/all_gather | solution.py:110
  108.0 2.4 fusion.1
  110.5 1.4 fusion.17
  113.5 79.5 %all-to-all-done.1 = bf16[64,144,128]{2,1,0:T(8,128)(2,1)S(1)} async-done(((bf16[64,144,128]{2,1,0:T(8,128)(2,1)}), bf16[64,144,128]{2,1,0:T(8,128)(2,1)S(1)}, u32[]{:S(2)}, u32[]{:S(2)}) %all-to-all-start.1) | async-done | bytes 2359328 | tf_op jit(solution)/shard_map/all_to_all | solution.py:95
  194.6 1.8 pad_maximum_fusion
  198.0 3.9 %convolution_convert_fusion.4 = bf16[33,32,128]{2,1,0:T(8,128)(2,1)} fusion(bf16[33,102,256]{2,1,0:T(8,128)(2,1)} %copy-done.8, f32[33,32]{1,0:T(8,128)S(1)} %fusion.87, f32[33,32,102]{2,1,0:T(8,128)S(1)} %fusion.22), kind=kOutput, calls=%fused_computation.33 | convolution fusion | flops 28033732 | bytes 2250752 | tf_op jit(solution)/shard_map/sqk,skd->sqd/dot_general | solution.py:163
  202.2 1.0 bitcast_convert_fusion.8
  203.2 1.0 slice.146
  205.8 6.0 %copy.49 = f32[33,32,8,128]{3,2,1,0:T(8,128)} copy(f32[33,32,8,128]{3,1,0,2:T(8,128)S(1)} %convert_bitcast_fusion) | data formatting | bytes 8650752 | tf_op jit(solution)/shard_map/convert_element_type | solution.py:115
  211.8 24.2 %all-gather.15.cloned.1.call-done = bf16[264,32,128]{2,1,0:T(8,128)(2,1)} async-done(((bf16[33,32,128]{2,1,0:T(8,128)(2,1)}), bf16[264,32,128]{2,1,0:T(8,128)(2,1)}) %all-gather.15.cloned.1.call-update) | async-done | bytes 2162704 | tf_op jit(solution)/shard_map/all_gather | solution.py:167
  236.0 6.0 %fusion.86 = (f32[1056]{0:T(1024)S(1)}, f32[1056]{0:T(1024)S(1)}, f32[1056,1024]{1,0:T(8,128)S(1)}) fusion(bf16[8,1056,128]{2,1,0:T(8,128)(2,1)} %bitcast.116, bf16[8,128,1024]{2,1,0:T(8,128)(2,1)S(1)} %bitcast.117, f32[132,8,8,128]{3,2,1,0:T(8,128)} %bitcast.109), kind=kOutput, calls=%fused_computation.148 | convolution fusion | flops 2218915840 | bytes 12919040 | tf_op jit(solution)/shard_map/grc,gcn->rn/dot_general | solution.py:169
  242.8 1.1 copy-done.3
  244.7 1.4 multiply_convert_fusion.3
  247.3 1.9 fusion.16
  250.1 29.7 %all-gather.17.cloned.1.call-done = bf16[264,32,128]{2,1,0:T(8,128)(2,1)} async-done(((bf16[33,32,128]{2,1,0:T(8,128)(2,1)}), bf16[264,32,128]{2,1,0:T(8,128)(2,1)}) %all-gather.17.cloned.1.call-update) | async-done | bytes 2162704 | tf_op jit(solution)/shard_map/all_gather | solution.py:194
  279.8 2.4 fusion.2
  (103 shorter events, 19.5 us)
Async XLA Ops:
  7.2 103.3 %copy-start = (bf16[1024,1,384]{2,0,1:T(8,128)(2,1)S(1)}, bf16[1024,1,384]{2,0,1:T(8,128)(2,1)}, u32[]{:S(2)}) copy-start(bf16[1024,1,384]{2,0,1:T(8,128)(2,1)} %param.24) | copy-start | bytes 2359300
  13.6 58.9 %all-to-all-start = ((bf16[64,48,128]{2,1,0:T(8,128)(2,1)}), bf16[64,48,128]{2,1,0:T(8,128)(2,1)S(1)}, u32[]{:S(2)}, u32[]{:S(2)}) async-start(bf16[64,48,128]{2,1,0:T(8,128)(2,1)} %copy.46), calls=%async_computation | async-start | bytes 1572864 | tf_op jit(solution)/shard_map/all_to_all | solution.py:80
  32.8 72.7 %all-gather.13.cloned.1.call-start = ((), (), s32[]{:S(2)}) async-start(), calls=%async_computation.4 | async-start | bytes 2433024 | tf_op jit(solution)/shard_map/all_gather | solution.py:110
  72.6 3.6 %copy-start.6 = (bf16[64,48,128]{2,1,0:T(8,128)(2,1)}, bf16[64,48,128]{2,1,0:T(8,128)(2,1)S(1)}, u32[]{:S(2)}) copy-start(bf16[64,48,128]{2,1,0:T(8,128)(2,1)S(1)} %all-to-all-done) | copy-start | bytes 2359300
  74.9 118.1 %copy-start.12 = (s32[64]{0:T(128)}, s32[64]{0:T(128)S(1)}, u32[]{:S(2)}) copy-start(s32[64]{0:T(128)S(1)} %get-tuple-element.33) | copy-start | bytes 772
  80.8 26.3 %copy-start.11 = (s32[33]{0:T(128)S(1)}, s32[33]{0:T(128)}, u32[]{:S(2)}) copy-start(s32[33]{0:T(128)} %param.19) | copy-start | bytes 400
  80.8 112.1 %all-to-all-start.1 = ((bf16[64,144,128]{2,1,0:T(8,128)(2,1)}), bf16[64,144,128]{2,1,0:T(8,128)(2,1)S(1)}, u32[]{:S(2)}, u32[]{:S(2)}) async-start(bf16[64,144,128]{2,1,0:T(8,128)(2,1)} %copy.52), calls=%async_computation.1 | async-start | bytes 4718592 | tf_op jit(solution)/shard_map/all_to_all | solution.py:95
  90.4 20.1 %copy-start.20 = (f32[1024]{0:T(1024)S(1)}, f32[1024]{0:T(1024)}, u32[]{:S(2)}) copy-start(f32[1024]{0:T(1024)} %param.23) | copy-start | bytes 12292
  90.4 104.1 %all-gather.9.cloned.1.call-start = ((), (), s32[]{:S(2)}) async-start(), calls=%async_computation.2 | async-start | bytes 2359296 | tf_op jit(solution)/shard_map/all_gather | solution.py:112
  105.5 89.1 %all-gather.11.cloned.1.call-start = ((), (), s32[]{:S(2)}) async-start(), calls=%async_computation.3 | async-start | bytes 2359296 | tf_op jit(solution)/shard_map/all_gather | solution.py:113
  106.2 129.8 %all-gather.15.cloned.1.call-start = ((), (), s32[]{:S(2)}) async-start(), calls=%async_computation.5 | async-start | bytes 2433024 | tf_op jit(solution)/shard_map/all_gather | solution.py:167
  106.4 4.1 %copy-start.1 = (bf16[264,32,128]{2,1,0:T(8,128)(2,1)S(1)}, bf16[264,32,128]{2,1,0:T(8,128)(2,1)}, u32[]{:S(2)}) copy-start(bf16[264,32,128]{2,1,0:T(8,128)(2,1)} %all-gather.13.cloned.1.call-done) | copy-start | bytes 6488068
  106.5 86.5 %copy-start.16 = (s32[32]{0:T(128)}, s32[32]{0:T(128)S(1)}, u32[]{:S(2)}) copy-start(s32[32]{0:T(128)S(1)} %iota_add_fusion.2) | copy-start | bytes 388
  194.5 2.5 copy-start.4
  194.5 1.9 copy-start.10
  197.6 4.6 %slice-start.1 = ((bf16[33,8,128]{2,1,0:T(8,128)(2,1)}), bf16[1,8,128]{2,1,0:T(8,128)(2,1)S(1)}, s32[]{:S(2)}) async-start(bf16[33,8,128]{2,1,0:T(8,128)(2,1)} %param.21), calls=%async_computation.8 | async-start | bytes 4096 | tf_op jit(solution)/shard_map/slice | solution.py:144
  198.0 7.2 %copy-start.2 = (bf16[264,32,128]{2,1,0:T(8,128)(2,1)S(1)}, bf16[264,32,128]{2,1,0:T(8,128)(2,1)}, u32[]{:S(2)}) copy-start(bf16[264,32,128]{2,1,0:T(8,128)(2,1)} %all-gather.13.cloned.1.call-done) | copy-start | bytes 6488068
  201.9 77.9 %all-gather.17.cloned.1.call-start = ((), (), s32[]{:S(2)}) async-start(), calls=%async_computation.6 | async-start | bytes 2433024 | tf_op jit(solution)/shard_map/all_gather | solution.py:194
  205.8 30.2 %copy-start.19 = (bf16[1024,1024]{1,0:T(8,128)(2,1)S(1)}, bf16[1024,1024]{1,0:T(8,128)(2,1)}, u32[]{:S(2)}) copy-start(bf16[1024,1024]{1,0:T(8,128)(2,1)} %all-gather.9.cloned.1.call-done) | copy-start | bytes 6291460
  236.0 6.0 %copy-start.9 = (bf16[1024,2,128]{2,1,0:T(2,128)(2,1)S(1)}, bf16[1024,2,128]{2,1,0:T(2,128)(2,1)}, u32[]{:S(2)}) copy-start(bf16[1024,2,128]{2,1,0:T(2,128)(2,1)} %param.27) | copy-start | bytes 1572868
  236.0 6.0 %copy-start.13 = (f32[1024]{0:T(1024)S(1)}, f32[1024]{0:T(1024)}, u32[]{:S(2)}) copy-start(f32[1024]{0:T(1024)} %param.26) | copy-start | bytes 12292
  242.0 2.0 copy-start.3
  244.6 2.6 copy-start.5
  244.6 2.6 copy-start.7
  (6 other events, 6.4 us)
Sparse Core Ops, SparseCore 0:
  76.2 29.1 all-gather.12
  107.6 33.4 all-gather.8
  143.2 33.2 all-gather.10
  202.1 33.8 all-gather.14
  246.2 33.5 all-gather.16
